TPU v7x, 128 devices: a whole 4x4x4 slice. The times are simulated.
128 devices in a mesh: outer: 16 (over z_hi, y, core), inner: 8 (over x, z_lo).
Axes of the slice: x: 4, y: 4, z: 4 (z_hi: 2, z_lo: 2; z = z_hi * 2 + z_lo), core: 2. Of those that a mesh axis runs over, the one named last changes fastest.
Arguments:
- q_load: bfloat16 [131072, 512], P(('outer', 'inner')), may hold values from -8 to 8
- kv_load: bfloat16 [131072, 256], P(('outer', 'inner')), may hold values from -8 to 8
- pack_dest: int32 [128, 8], P('outer'), may hold values from -1 to 31, as said below
- counts: int32 [128], P('outer'), may hold values from 0 to 8, as said below
- segment_ids: int32 [65536], P(('outer', 'inner')), may hold values from 0 to 7, never falling along the last dimension, each value on 1 to 16384 neighbouring positions
Outputs:
- attn_out: bfloat16 [65536, 512], P(('outer', 'inner'))
Inputs may be any that keep to these rules, and one draw needn't show every extreme that they name: In each group of 8 loader shards that share an outer index the counts add up to 32; some shard of every group holds 8 live blocks and some holds none. `pack_dest`: live entries of a group name every block number 0 to 31 exactly once; block number t goes to the device of inner index t // 4 in the same group, as its block t % 4; a shard sends at most 1 block to one device, and some shard sends exactly 1; entries of slots that are not live are -1. `segment_ids`: never falling along the sequence.
All inputs are finite; a program needn't handle non-finite values.
Results may differ from a plain program's by a relative error of at most 0.0059.
Values may be sent and summed in bfloat16 or wider, within the bound.
No kernel may reach another device: no remote copies, remote signals or barrier semaphores. Data moves between devices by JAX's collectives and lax.ppermute only.
A program may use at most 64 MiB of HBM per device.

v0:
```python
import math

import jax
import jax.numpy as jnp
from jax import lax
from jax.experimental import pallas as pl
from jax.experimental.pallas import tpu as pltpu
from jax.sharding import PartitionSpec as P


def shifted(value, axis, steps):
    count = lax.axis_size(axis)
    leading, last = (max(0, -steps), min(count, count - steps))
    return lax.ppermute(value, axis, [(source, source + steps) for source in range(leading, last)])


def select_rows(selector, blocks, pattern):
    return jnp.einsum(
        pattern, selector.astype(jnp.bfloat16), blocks, preferred_element_type=jnp.float32
    ).astype(jnp.bfloat16)


def local(q_load, kv_load, pack_dest, counts, segment_ids):
    group_width = lax.axis_size("inner")
    my_index = lax.axis_index("inner")
    capacity = pack_dest.shape[1]
    slot_count = capacity // 2
    pair_limit = -(-capacity // group_width)
    row_length = q_load.shape[0] // capacity
    query_width = q_load.shape[1]
    pair_width = kv_load.shape[1]
    head_size = pair_width // 2
    head_count = query_width // head_size
    slot_grid = lax.broadcasted_iota(jnp.int32, (group_width, capacity), 1)
    live_all = slot_grid < counts[:, None]
    owner_all = pack_dest // slot_count
    slot_numbers = jnp.arange(capacity, dtype=jnp.int32)
    earlier = slot_numbers[None, :] < slot_numbers[:, None]
    same_owner = owner_all[:, :, None] == owner_all[:, None, :]
    rank_all = jnp.sum(
        (earlier[None] & same_owner & live_all[:, None, :]).astype(jnp.int32), axis=2
    )
    shard_rows = jnp.arange(group_width, dtype=jnp.int32)
    mine_row = (shard_rows == my_index)[:, None]
    my_owner = jnp.sum(jnp.where(mine_row, owner_all, 0), axis=0)
    my_rank = jnp.sum(jnp.where(mine_row, rank_all, 0), axis=0)
    my_live = jnp.any(mine_row & live_all, axis=0)
    pair_ids = jnp.arange(pair_limit, dtype=jnp.int32)
    send_select = (
        my_live[None, None, :]
        & (my_owner[None, None, :] == shard_rows[:, None, None])
        & (my_rank[None, None, :] == pair_ids[None, :, None])
    )
    q_blocks = q_load.reshape(capacity, row_length, query_width)
    kv_blocks = kv_load.reshape(capacity, row_length, pair_width)
    send_q = select_rows(send_select, q_blocks, "jkc,crf->jkrf")
    send_kv = select_rows(send_select, kv_blocks, "jkc,crf->jkrf")
    recv_both = lax.all_to_all(
        jnp.concatenate([send_q, send_kv], axis=3), "inner", split_axis=0, concat_axis=0, tiled=True
    )
    recv_q = recv_both[..., :query_width]
    recv_kv = recv_both[..., query_width:]
    wanted = my_index * slot_count + jnp.arange(slot_count, dtype=jnp.int32)
    take_select = jnp.any(
        live_all[None, :, None, :]
        & (pack_dest[None, :, None, :] == wanted[:, None, None, None])
        & (rank_all[None, :, None, :] == pair_ids[None, None, :, None]),
        axis=3,
    )
    q_seq = select_rows(take_select, recv_q, "srk,rktf->stf").reshape(
        slot_count * row_length, query_width
    )
    kv_seq = select_rows(take_select, recv_kv, "srk,rktf->stf").reshape(
        slot_count * row_length, pair_width
    )
    tok_rows = q_seq.shape[0]
    owner_index = lax.axis_index(("outer", "inner"))
    outer_index = lax.axis_index("outer")
    score_scale = 1.0 / math.sqrt(head_size)
    extra_rows = 16
    seg_rows = tok_rows // pair_width
    seg_pad = jnp.zeros((extra_rows - seg_rows, pair_width), jnp.bfloat16)
    packed = jnp.concatenate(
        [kv_seq, segment_ids.astype(jnp.bfloat16).reshape(seg_rows, pair_width), seg_pad], axis=0
    )
    outer_reach = -(-(lax.axis_size("outer") * group_width // 4) // group_width)
    own_steps = list(range(0, outer_reach + 1, 2))
    partner_steps = list(range(1, outer_reach + 1, 2))
    moved = [packed if step == 0 else shifted(packed, "outer", step) for step in own_steps]
    own_stack = jnp.stack(moved)
    inner_shifts = [own_stack] + [
        lax.ppermute(own_stack, "inner", [(i, (i + s) % group_width) for i in range(group_width)])
        for s in range(1, group_width)
    ]
    gathered = jnp.stack(inner_shifts)
    inner_of = (my_index - jnp.arange(group_width, dtype=jnp.int32)) % group_width
    parity = outer_index % 2
    offer = lax.dynamic_slice_in_dim(gathered, parity, len(partner_steps), axis=1)
    outer_count = lax.axis_size("outer")
    partner_pairs = [(o, o ^ 1) for o in range(outer_count)]
    received = lax.ppermute(offer, "outer", partner_pairs)
    sources = [(gathered, own_steps), (received, partner_steps)]
    key_device, key_first, key_last = [], [], []
    for array, steps in sources:
        for slot, step in enumerate(steps):
            key_device.append(
                (outer_index - step) * group_width + inner_of
            )
            key_first.append(array[:, slot, tok_rows, 0])
            key_last.append(array[:, slot, tok_rows + seg_rows - 1, pair_width - 1])
    key_device = jnp.concatenate(key_device)
    key_first = jnp.concatenate(key_first)
    key_last = jnp.concatenate(key_last)
    first_seg = segment_ids[0].astype(jnp.bfloat16)
    last_seg = segment_ids[tok_rows - 1].astype(jnp.bfloat16)
    needed = (
        (key_device >= 0)
        & (key_device <= owner_index)
        & (key_last >= first_seg)
        & (key_first <= last_seg)
    ).astype(jnp.int32)
    meta = jnp.concatenate([owner_index.reshape(1).astype(jnp.int32), needed, key_device])
    query_seg = segment_ids.astype(jnp.float32).reshape(tok_rows, 1)
    return attend(meta, q_seq, query_seg, gathered, received, head_count, head_size, score_scale)


def attend(meta, q_seq, query_seg, gathered, received, head_count, head_size, score_scale):
    tok_rows = q_seq.shape[0]
    group_width, first_slots, packed_rows, pair_width = gathered.shape
    second_slots = received.shape[1]
    first_count = group_width * first_slots
    block_count = first_count + group_width * second_slots
    seg_rows = tok_rows // pair_width

    def kernel(meta_ref, q_ref, qseg_ref, first_ref, second_ref, out_ref, m_ref, l_ref, acc_ref):
        b = pl.program_id(0)

        @pl.when(b == 0)
        def _():
            m_ref[...] = jnp.full(m_ref.shape, -1e30, jnp.float32)
            l_ref[...] = jnp.zeros(l_ref.shape, jnp.float32)
            acc_ref[...] = jnp.zeros(acc_ref.shape, jnp.float32)

        def absorb(kv_ref):
            own = meta_ref[0]
            device = meta_ref[1 + block_count + b]
            seg_parts = [
                kv_ref[0, 0, tok_rows + r : tok_rows + r + 1, :].astype(jnp.float32)
                for r in range(seg_rows)
            ]
            key_seg = jnp.concatenate(seg_parts, axis=1)
            key_pos = device * tok_rows + lax.broadcasted_iota(jnp.int32, (1, tok_rows), 1)
            query_pos = own * tok_rows + lax.broadcasted_iota(jnp.int32, (tok_rows, 1), 0)
            visible = (key_pos <= query_pos) & (key_seg == qseg_ref[...])
            keys = kv_ref[0, 0, :tok_rows, :head_size]
            values = kv_ref[0, 0, :tok_rows, head_size:]
            for h in range(head_count):
                queries = q_ref[:, h * head_size : (h + 1) * head_size]
                scores = lax.dot_general(
                    queries, keys, (((1,), (1,)), ((), ())), preferred_element_type=jnp.float32
                ) * score_scale
                masked = jnp.where(visible, scores, -1e30)
                m_prev = m_ref[h]
                m_next = jnp.maximum(m_prev, jnp.max(masked, axis=1, keepdims=True))
                factor = jnp.exp(m_prev - m_next)
                weights = jnp.where(visible, jnp.exp(masked - m_next[:, :1]), 0.0)
                l_ref[h] = l_ref[h] * factor + jnp.sum(weights, axis=1, keepdims=True)
                acc_ref[h] = acc_ref[h] * factor + jnp.dot(
                    weights.astype(jnp.bfloat16), values, preferred_element_type=jnp.float32
                )
                m_ref[h] = m_next

        live = meta_ref[1 + b] == 1

        @pl.when(live & (b < first_count))
        def _():
            absorb(first_ref)

        @pl.when(live & (b >= first_count))
        def _():
            absorb(second_ref)

        @pl.when(b == block_count - 1)
        def _():
            for h in range(head_count):
                out_ref[:, h * head_size : (h + 1) * head_size] = (
                    acc_ref[h] / l_ref[h]
                ).astype(out_ref.dtype)

    def first_map(b, meta):
        c = jnp.minimum(b, first_count - 1)
        return (c % group_width, c // group_width, 0, 0)

    def second_map(b, meta):
        c = jnp.maximum(b - first_count, 0)
        return (c % group_width, c // group_width, 0, 0)

    grid_spec = pltpu.PrefetchScalarGridSpec(
        num_scalar_prefetch=1,
        grid=(block_count,),
        in_specs=[
            pl.BlockSpec(q_seq.shape, lambda b, meta: (0, 0)),
            pl.BlockSpec(query_seg.shape, lambda b, meta: (0, 0)),
            pl.BlockSpec((1, 1, packed_rows, pair_width), first_map),
            pl.BlockSpec((1, 1, packed_rows, pair_width), second_map),
        ],
        out_specs=pl.BlockSpec(q_seq.shape, lambda b, meta: (0, 0)),
        scratch_shapes=[
            pltpu.VMEM((head_count, tok_rows, head_size), jnp.float32),
            pltpu.VMEM((head_count, tok_rows, head_size), jnp.float32),
            pltpu.VMEM((head_count, tok_rows, head_size), jnp.float32),
        ],
    )
    flops = 4 * block_count * tok_rows * tok_rows * head_size * head_count
    return pl.pallas_call(
        kernel,
        grid_spec=grid_spec,
        out_shape=jax.ShapeDtypeStruct(q_seq.shape, q_seq.dtype),
        compiler_params=pltpu.CompilerParams(dimension_semantics=("arbitrary",)),
        cost_estimate=pl.CostEstimate(
            flops=flops,
            transcendentals=block_count * tok_rows * tok_rows * head_count,
            bytes_accessed=(gathered.size + received.size) * 2 + q_seq.size * 4,
        ),
    )(meta, q_seq, query_seg, gathered, received)


def solution(mesh):
    in_specs = (
        P(("outer", "inner"), None),
        P(("outer", "inner"), None),
        P("outer", None),
        P("outer"),
        P(("outer", "inner")),
    )
    out_specs = P(("outer", "inner"), None)
    return jax.shard_map(local, mesh=mesh, in_specs=in_specs, out_specs=out_specs, check_vma=False)
```

profile of v0, /device:TPU:127, one launch (start us, length us, event | category | flops | bytes accessed | tf_op | source)
XLA Modules:
  0.0 276.1 jit_solution(2247153617576616430)
XLA Ops:
  0.0 0.0 copy-start
  0.0 0.0 copy-start.2
  0.0 0.8 add_select_fusion
  0.8 0.7 and_reduce_fusion.1
  1.6 0.3 convert_reduce_fusion
  1.8 0.8 select_reduce_fusion
  2.6 0.0 copy-done
  2.6 0.7 fusion
  3.3 1.4 fusion.1
  4.8 0.1 pad_maximum_fusion
  4.9 1.4 copy.25
  6.3 5.1 %all-to-all-start = ((bf16[8,1,128,768]{3,2,1,0:T(8,128)(2,1)}), bf16[8,1,128,768]{3,2,1,0:T(8,128)(2,1)S(1)}, u32[]{:S(2)}, u32[]{:S(2)}) async-start(bf16[8,1,128,768]{3,2,1,0:T(8,128)(2,1)} %copy.25), calls=%async_computation | async-start | bytes 3145728 | tf_op jit(solution)/shard_map/all_to_all | solution.py:58
  11.4 0.0 copy-done.3
  11.5 0.1 pad.5.clone
  11.6 0.0 copy-done.2
  11.6 0.2 and_reduce_fusion
  11.8 18.6 %all-to-all-done = bf16[8,1,128,768]{3,2,1,0:T(8,128)(2,1)S(1)} async-done(((bf16[8,1,128,768]{3,2,1,0:T(8,128)(2,1)}), bf16[8,1,128,768]{3,2,1,0:T(8,128)(2,1)S(1)}, u32[]{:S(2)}, u32[]{:S(2)}) %all-to-all-start) | async-done | bytes 1572896 | tf_op jit(solution)/shard_map/all_to_all | solution.py:58
  30.4 0.4 convolution_convert_fusion.3
  30.9 0.1 fusion.20
  31.0 1.3 collective-permute-start
  32.3 1.3 collective-permute-start.1
  33.6 5.4 %collective-permute-done = bf16[528,256]{1,0:T(8,128)(2,1)S(1)} collective-permute-done((bf16[528,256]{1,0:T(8,128)(2,1)S(1)}, bf16[528,256]{1,0:T(8,128)(2,1)S(1)}, u32[]{:S(2)}, u32[]{:S(2)}) %collective-permute-start) | collective-permute-done | bytes 270368 | tf_op jit(solution)/shard_map/ppermute | solution.py:14
  39.1 2.8 %collective-permute-done.1 = bf16[528,256]{1,0:T(8,128)(2,1)S(1)} collective-permute-done((bf16[528,256]{1,0:T(8,128)(2,1)S(1)}, bf16[528,256]{1,0:T(8,128)(2,1)S(1)}, u32[]{:S(2)}, u32[]{:S(2)}) %collective-permute-start.1) | collective-permute-done | bytes 270368 | tf_op jit(solution)/shard_map/ppermute | solution.py:14
  41.9 1.0 pad_maximum_fusion.1
  42.9 4.3 %collective-permute-start.2 = (bf16[3,528,256]{2,1,0:T(8,128)(2,1)}, bf16[3,528,256]{2,1,0:T(8,128)(2,1)}, u32[]{:S(2)}, u32[]{:S(2)}) collective-permute-start(bf16[3,528,256]{2,1,0:T(8,128)(2,1)} %pad_maximum_fusion.1), channel_id=1, source_target_pairs={{0,1},{1,2},{2,3},{3,4},{4,5},{5,6},{6,7},{7,0},{8,9},{9,10},{10,1... | collective-permute-start | bytes 2433032 | tf_op jit(solution)/shard_map/ppermute | solution.py:92
  47.1 0.0 collective-permute-start.3
  47.1 0.3 collective-permute-start.4
  47.4 2.7 collective-permute-start.5
  50.1 0.1 bitcast_dynamic-update-slice_fusion.7
  50.2 0.1 collective-permute-start.6
  50.3 12.0 %collective-permute-done.2 = bf16[3,528,256]{2,1,0:T(8,128)(2,1)} collective-permute-done((bf16[3,528,256]{2,1,0:T(8,128)(2,1)}, bf16[3,528,256]{2,1,0:T(8,128)(2,1)}, u32[]{:S(2)}, u32[]{:S(2)}) %collective-permute-start.2) | collective-permute-done | bytes 811040 | tf_op jit(solution)/shard_map/ppermute | solution.py:92
  62.3 10.0 %collective-permute-start.7 = (bf16[3,528,256]{2,1,0:T(8,128)(2,1)}, bf16[3,528,256]{2,1,0:T(8,128)(2,1)S(1)}, u32[]{:S(2)}, u32[]{:S(2)}) collective-permute-start(bf16[3,528,256]{2,1,0:T(8,128)(2,1)} %pad_maximum_fusion.1), channel_id=1, source_target_pairs={{0,6},{1,7},{2,0},{3,1},{4,2},{5,3},{6,4},{7,5},{8,14},{9,15},{10,... | collective-permute-start | bytes 2433032 | tf_op jit(solution)/shard_map/ppermute | solution.py:92
  72.3 1.2 bitcast_dynamic-update-slice_fusion.6
  73.5 17.8 %collective-permute-done.3 = bf16[3,528,256]{2,1,0:T(8,128)(2,1)} collective-permute-done((bf16[3,528,256]{2,1,0:T(8,128)(2,1)}, bf16[3,528,256]{2,1,0:T(8,128)(2,1)}, u32[]{:S(2)}, u32[]{:S(2)}) %collective-permute-start.3) | collective-permute-done | bytes 811040 | tf_op jit(solution)/shard_map/ppermute | solution.py:92
  91.3 0.0 collective-permute-start.8
  91.3 1.2 bitcast_dynamic-update-slice_fusion.5
  92.5 0.1 collective-permute-done.4
  92.6 1.2 bitcast_dynamic-update-slice_fusion.4
  93.8 8.3 %collective-permute-done.5 = bf16[3,528,256]{2,1,0:T(8,128)(2,1)S(1)} collective-permute-done((bf16[3,528,256]{2,1,0:T(8,128)(2,1)}, bf16[3,528,256]{2,1,0:T(8,128)(2,1)S(1)}, u32[]{:S(2)}, u32[]{:S(2)}) %collective-permute-start.5) | collective-permute-done | bytes 811040 | tf_op jit(solution)/shard_map/ppermute | solution.py:92
  102.1 0.1 bitcast_dynamic-update-slice_fusion.3
  102.1 30.3 %collective-permute-done.6 = bf16[3,528,256]{2,1,0:T(8,128)(2,1)S(1)} collective-permute-done((bf16[3,528,256]{2,1,0:T(8,128)(2,1)}, bf16[3,528,256]{2,1,0:T(8,128)(2,1)S(1)}, u32[]{:S(2)}, u32[]{:S(2)}) %collective-permute-start.6) | collective-permute-done | bytes 811040 | tf_op jit(solution)/shard_map/ppermute | solution.py:92
  132.4 0.1 bitcast_dynamic-update-slice_fusion.2
  132.5 17.4 %collective-permute-done.7 = bf16[3,528,256]{2,1,0:T(8,128)(2,1)S(1)} collective-permute-done((bf16[3,528,256]{2,1,0:T(8,128)(2,1)}, bf16[3,528,256]{2,1,0:T(8,128)(2,1)S(1)}, u32[]{:S(2)}, u32[]{:S(2)}) %collective-permute-start.7) | collective-permute-done | bytes 811040 | tf_op jit(solution)/shard_map/ppermute | solution.py:92
  149.8 0.1 bitcast_dynamic-update-slice_fusion.1
  149.9 0.0 collective-permute-done.8
  149.9 0.1 bitcast_dynamic-update-slice_fusion.first_ref
  150.0 0.0 copy-start.1
  150.0 2.7 copy-done.1
  152.7 2.4 constant_dynamic-slice_fusion
  155.1 2.9 %collective-permute-start.9 = (bf16[8,2,528,256]{3,2,1,0:T(8,128)(2,1)}, bf16[8,2,528,256]{3,2,1,0:T(8,128)(2,1)}, u32[]{:S(2)}, u32[]{:S(2)}) collective-permute-start(bf16[8,2,528,256]{3,2,1,0:T(8,128)(2,1)} %constant_dynamic-slice_fusion), channel_id=1, source_target_pairs={{0,8},{8,0},{16,24},{24,16},{32,40},{40,32},{48,56},{56,48},{64,72... | collective-permute-start | bytes 12976136 | tf_op jit(solution)/shard_map/ppermute | solution.py:101
  157.9 0.9 copy.30.qseg_ref
  158.8 0.1 concatenate.19
  158.9 0.6 fusion.22
  159.5 0.1 slice.69
  159.6 0.7 convolution_convert_fusion.1
  160.3 0.9 copy.29
  161.2 1.0 slice_reduce_fusion.7
  162.3 3.0 %collective-permute-done.9.second_ref = bf16[8,2,528,256]{3,2,1,0:T(8,128)(2,1)} collective-permute-done((bf16[8,2,528,256]{3,2,1,0:T(8,128)(2,1)}, bf16[8,2,528,256]{3,2,1,0:T(8,128)(2,1)}, u32[]{:S(2)}, u32[]{:S(2)}) %collective-permute-start.9) | collective-permute-done | bytes 4325408 | tf_op jit(solution)/shard_map/ppermute | solution.py:101
  165.3 1.0 slice_reduce_fusion.5
  166.2 0.1 concatenate.22
  166.3 0.1 concatenate.23
  166.4 1.2 and_convert_fusion
  167.7 0.6 concatenate.24.meta_ref
  168.3 107.8 %shard_map.55 = bf16[512,512]{1,0:T(8,128)(2,1)} custom-call(s32[81]{0:T(128)} %concatenate.24.meta_ref, bf16[512,512]{1,0:T(8,128)(2,1)} %bitcast.56, f32[512,1]{1,0:T(8,128)} %copy.30.qseg_ref, bf16[8,3,528,256]{3,2,1,0:T(8,128)(2,1)} %copy-done.1, bf16[8,2,528,256]{3,2,1,0:T(8,128)(2,1)} %collective-permute-done.9.second_ref), custom_call_target="tpu_custom_call" | custom-call | flops 21474836480 | bytes 11862016 | tf_op jit(solution)/shard_map/pallas_call | solution.py:215
  (13 shorter events, 0.1 us)
Async XLA Ops:
  0.0 2.6 copy-start
  0.0 11.6 %copy-start.2 = (s32[8,8]{1,0:T(8,128)S(1)}, s32[8,8]{1,0:T(8,128)}, u32[]{:S(2)}) copy-start(s32[8,8]{1,0:T(8,128)} %param.7) | copy-start | bytes 772
  0.0 11.4 %copy-start.3 = (s32[512]{0:T(512)S(1)}, s32[512]{0:T(512)}, u32[]{:S(2)}) copy-start(s32[512]{0:T(512)} %param.9) | copy-start | bytes 6148
  6.3 24.1 %all-to-all-start = ((bf16[8,1,128,768]{3,2,1,0:T(8,128)(2,1)}), bf16[8,1,128,768]{3,2,1,0:T(8,128)(2,1)S(1)}, u32[]{:S(2)}, u32[]{:S(2)}) async-start(bf16[8,1,128,768]{3,2,1,0:T(8,128)(2,1)} %copy.25), calls=%async_computation | async-start | bytes 3145728 | tf_op jit(solution)/shard_map/all_to_all | solution.py:58
  31.0 8.0 %collective-permute-start = (bf16[528,256]{1,0:T(8,128)(2,1)S(1)}, bf16[528,256]{1,0:T(8,128)(2,1)S(1)}, u32[]{:S(2)}, u32[]{:S(2)}) collective-permute-start(bf16[528,256]{1,0:T(8,128)(2,1)S(1)} %get-tuple-element.18), channel_id=1, source_target_pairs={{0,16},{8,24},{16,32},{24,40},{32,48},{40,56},{48,64},{56,72},{64,... | collective-permute-start | bytes 811016 | tf_op jit(solution)/shard_map/ppermute | solution.py:14
  32.3 9.5 %collective-permute-start.1 = (bf16[528,256]{1,0:T(8,128)(2,1)S(1)}, bf16[528,256]{1,0:T(8,128)(2,1)S(1)}, u32[]{:S(2)}, u32[]{:S(2)}) collective-permute-start(bf16[528,256]{1,0:T(8,128)(2,1)S(1)} %get-tuple-element.18), channel_id=1, source_target_pairs={{0,32},{8,40},{16,48},{24,56},{32,64},{40,72},{48,80},{56,88},{64,... | collective-permute-start | bytes 811016 | tf_op jit(solution)/shard_map/ppermute | solution.py:14
  42.9 19.4 %collective-permute-start.2 = (bf16[3,528,256]{2,1,0:T(8,128)(2,1)}, bf16[3,528,256]{2,1,0:T(8,128)(2,1)}, u32[]{:S(2)}, u32[]{:S(2)}) collective-permute-start(bf16[3,528,256]{2,1,0:T(8,128)(2,1)} %pad_maximum_fusion.1), channel_id=1, source_target_pairs={{0,1},{1,2},{2,3},{3,4},{4,5},{5,6},{6,7},{7,0},{8,9},{9,10},{10,1... | collective-permute-start | bytes 2433032 | tf_op jit(solution)/shard_map/ppermute | solution.py:92
  47.1 44.2 %collective-permute-start.3 = (bf16[3,528,256]{2,1,0:T(8,128)(2,1)}, bf16[3,528,256]{2,1,0:T(8,128)(2,1)}, u32[]{:S(2)}, u32[]{:S(2)}) collective-permute-start(bf16[3,528,256]{2,1,0:T(8,128)(2,1)} %pad_maximum_fusion.1), channel_id=1, source_target_pairs={{0,2},{1,3},{2,4},{3,5},{4,6},{5,7},{6,0},{7,1},{8,10},{9,11},{10,... | collective-permute-start | bytes 2433032 | tf_op jit(solution)/shard_map/ppermute | solution.py:92
  47.1 45.4 %collective-permute-start.4 = (bf16[3,528,256]{2,1,0:T(8,128)(2,1)}, bf16[3,528,256]{2,1,0:T(8,128)(2,1)}, u32[]{:S(2)}, u32[]{:S(2)}) collective-permute-start(bf16[3,528,256]{2,1,0:T(8,128)(2,1)} %pad_maximum_fusion.1), channel_id=1, source_target_pairs={{0,3},{1,4},{2,5},{3,6},{4,7},{5,0},{6,1},{7,2},{8,11},{9,12},{10,... | collective-permute-start | bytes 2433032 | tf_op jit(solution)/shard_map/ppermute | solution.py:92
  47.4 54.7 %collective-permute-start.5 = (bf16[3,528,256]{2,1,0:T(8,128)(2,1)}, bf16[3,528,256]{2,1,0:T(8,128)(2,1)S(1)}, u32[]{:S(2)}, u32[]{:S(2)}) collective-permute-start(bf16[3,528,256]{2,1,0:T(8,128)(2,1)} %pad_maximum_fusion.1), channel_id=1, source_target_pairs={{0,4},{1,5},{2,6},{3,7},{4,0},{5,1},{6,2},{7,3},{8,12},{9,13},{10,... | collective-permute-start | bytes 2433032 | tf_op jit(solution)/shard_map/ppermute | solution.py:92
  50.2 82.2 %collective-permute-start.6 = (bf16[3,528,256]{2,1,0:T(8,128)(2,1)}, bf16[3,528,256]{2,1,0:T(8,128)(2,1)S(1)}, u32[]{:S(2)}, u32[]{:S(2)}) collective-permute-start(bf16[3,528,256]{2,1,0:T(8,128)(2,1)} %pad_maximum_fusion.1), channel_id=1, source_target_pairs={{0,5},{1,6},{2,7},{3,0},{4,1},{5,2},{6,3},{7,4},{8,13},{9,14},{10,... | collective-permute-start | bytes 2433032 | tf_op jit(solution)/shard_map/ppermute | solution.py:92
  62.3 87.6 %collective-permute-start.7 = (bf16[3,528,256]{2,1,0:T(8,128)(2,1)}, bf16[3,528,256]{2,1,0:T(8,128)(2,1)S(1)}, u32[]{:S(2)}, u32[]{:S(2)}) collective-permute-start(bf16[3,528,256]{2,1,0:T(8,128)(2,1)} %pad_maximum_fusion.1), channel_id=1, source_target_pairs={{0,6},{1,7},{2,0},{3,1},{4,2},{5,3},{6,4},{7,5},{8,14},{9,15},{10,... | collective-permute-start | bytes 2433032 | tf_op jit(solution)/shard_map/ppermute | solution.py:92
  91.3 58.6 %collective-permute-start.8 = (bf16[3,528,256]{2,1,0:T(8,128)(2,1)}, bf16[3,528,256]{2,1,0:T(8,128)(2,1)S(1)}, u32[]{:S(2)}, u32[]{:S(2)}) collective-permute-start(bf16[3,528,256]{2,1,0:T(8,128)(2,1)} %pad_maximum_fusion.1), channel_id=1, source_target_pairs={{0,7},{1,0},{2,1},{3,2},{4,3},{5,4},{6,5},{7,6},{8,15},{9,8},{10,9... | collective-permute-start | bytes 2433032 | tf_op jit(solution)/shard_map/ppermute | solution.py:92
  150.0 2.7 copy-start.1
  155.1 10.2 %collective-permute-start.9 = (bf16[8,2,528,256]{3,2,1,0:T(8,128)(2,1)}, bf16[8,2,528,256]{3,2,1,0:T(8,128)(2,1)}, u32[]{:S(2)}, u32[]{:S(2)}) collective-permute-start(bf16[8,2,528,256]{3,2,1,0:T(8,128)(2,1)} %constant_dynamic-slice_fusion), channel_id=1, source_target_pairs={{0,8},{8,0},{16,24},{24,16},{32,40},{40,32},{48,56},{56,48},{64,72... | collective-permute-start | bytes 12976136 | tf_op jit(solution)/shard_map/ppermute | solution.py:101
where the time goes:
time: 277 us; the launch traced here: 276 us
  waiting for transfers between devices  116 us (42%)
  Pallas kernels  108 us (39%)
  starting transfers between devices  27.9 us (10%)
  local copies, waits for them, and re-layouts  15.8 us (6%)
  other arithmetic  5.34 us (2%)
  matrix products  3.28 us (1%)
    pallas_call x1, Pallas kernels, attend(): pl.pallas_call(kernel, grid_spec=grid_spec, out_shape=jax.ShapeDtypeStruc...  108 us
    ppermute x7, waiting for transfers between devices, local(): lax.ppermute(own_stack, 'inner', [(i, (i + s) % group_width) for i in ran...  85.9 us
    all_to_all x1, waiting for transfers between devices, local(): lax.all_to_all(jnp.concatenate([send_q, send_kv], axis=3), 'inner', split...  18.6 us
    ppermute x7, starting transfers between devices, local(): lax.ppermute(own_stack, 'inner', [(i, (i + s) % group_width) for i in ran...  17.3 us
    ppermute x2, waiting for transfers between devices, shifted(): lax.ppermute(value, axis, [(source, source + steps) for source in range(l...  8.25 us
    unnamed x14, local copies, waits for them, and re-layouts  6.46 us
  transfers between devices with their start and end apart: 11, of which 10 were waited for; matrix products, arithmetic and copies ran while one was open for 3% of the time, Pallas kernels for 0%

commit v1 on v0

--- a/solution.py
+++ b/solution.py
@@ -118,7 +118,14 @@
         & (key_device <= owner_index)
         & (key_last >= first_seg)
         & (key_first <= last_seg)
-    ).astype(jnp.int32)
+    )
+    whole = (
+        (key_device < owner_index)
+        & (key_first == key_last)
+        & (key_first == first_seg)
+        & (first_seg == last_seg)
+    )
+    needed = jnp.where(needed, jnp.where(whole, 1, 2), 0).astype(jnp.int32)
     meta = jnp.concatenate([owner_index.reshape(1).astype(jnp.int32), needed, key_device])
     query_seg = segment_ids.astype(jnp.float32).reshape(tok_rows, 1)
     return attend(meta, q_seq, query_seg, gathered, received, head_count, head_size, score_scale)
@@ -141,44 +148,46 @@
             l_ref[...] = jnp.zeros(l_ref.shape, jnp.float32)
             acc_ref[...] = jnp.zeros(acc_ref.shape, jnp.float32)
 
-        def absorb(kv_ref):
-            own = meta_ref[0]
-            device = meta_ref[1 + block_count + b]
-            seg_parts = [
-                kv_ref[0, 0, tok_rows + r : tok_rows + r + 1, :].astype(jnp.float32)
-                for r in range(seg_rows)
-            ]
-            key_seg = jnp.concatenate(seg_parts, axis=1)
-            key_pos = device * tok_rows + lax.broadcasted_iota(jnp.int32, (1, tok_rows), 1)
-            query_pos = own * tok_rows + lax.broadcasted_iota(jnp.int32, (tok_rows, 1), 0)
-            visible = (key_pos <= query_pos) & (key_seg == qseg_ref[...])
+        def absorb(kv_ref, masked_block):
             keys = kv_ref[0, 0, :tok_rows, :head_size]
             values = kv_ref[0, 0, :tok_rows, head_size:]
+            if masked_block:
+                own = meta_ref[0]
+                device = meta_ref[1 + block_count + b]
+                seg_parts = [
+                    kv_ref[0, 0, tok_rows + r : tok_rows + r + 1, :].astype(jnp.float32)
+                    for r in range(seg_rows)
+                ]
+                key_seg = jnp.concatenate(seg_parts, axis=1)
+                key_pos = device * tok_rows + lax.broadcasted_iota(jnp.int32, (1, tok_rows), 1)
+                query_pos = own * tok_rows + lax.broadcasted_iota(jnp.int32, (tok_rows, 1), 0)
+                visible = (key_pos <= query_pos) & (key_seg == qseg_ref[...])
             for h in range(head_count):
                 queries = q_ref[:, h * head_size : (h + 1) * head_size]
                 scores = lax.dot_general(
                     queries, keys, (((1,), (1,)), ((), ())), preferred_element_type=jnp.float32
-                ) * score_scale
-                masked = jnp.where(visible, scores, -1e30)
+                )
+                if masked_block:
+                    scores = jnp.where(visible, scores, -1e30)
                 m_prev = m_ref[h]
-                m_next = jnp.maximum(m_prev, jnp.max(masked, axis=1, keepdims=True))
-                factor = jnp.exp(m_prev - m_next)
-                weights = jnp.where(visible, jnp.exp(masked - m_next[:, :1]), 0.0)
+                m_next = jnp.maximum(m_prev, jnp.max(scores, axis=1, keepdims=True))
+                factor = jnp.exp((m_prev - m_next) * score_scale)
+                m_row = m_next[:, :1]
+                if masked_block:
+                    m_row = jnp.where(m_row == -1e30, 0.0, m_row)
+                weights = jnp.exp((scores - m_row) * score_scale)
                 l_ref[h] = l_ref[h] * factor + jnp.sum(weights, axis=1, keepdims=True)
                 acc_ref[h] = acc_ref[h] * factor + jnp.dot(
                     weights.astype(jnp.bfloat16), values, preferred_element_type=jnp.float32
                 )
                 m_ref[h] = m_next
 
-        live = meta_ref[1 + b] == 1
-
-        @pl.when(live & (b < first_count))
-        def _():
-            absorb(first_ref)
-
-        @pl.when(live & (b >= first_count))
-        def _():
-            absorb(second_ref)
+        mode = meta_ref[1 + b]
+        for ref, in_range in ((first_ref, b < first_count), (second_ref, b >= first_count)):
+            for masked_block, code in ((False, 1), (True, 2)):
+                @pl.when(in_range & (mode == code))
+                def _(ref=ref, masked_block=masked_block):
+                    absorb(ref, masked_block)
 
         @pl.when(b == block_count - 1)
         def _():

time: 277 us -> 280 us (1.011)
  the two profiles are of different devices: /device:TPU:127 before, /device:TPU:53 now
where the time goes in v1:
time: 280 us; the launch traced here: 282 us
  waiting for transfers between devices  125 us (45%)
  Pallas kernels  107 us (38%)
  starting transfers between devices  23.4 us (8%)
  local copies, waits for them, and re-layouts  15.8 us (6%)
  other arithmetic  5.35 us (2%)
  matrix products  3.28 us (1%)
    pallas_call x1, Pallas kernels, attend(): pl.pallas_call(kernel, grid_spec=grid_spec, out_shape=jax.ShapeDtypeStruc...  107 us
    ppermute x7, waiting for transfers between devices, local(): lax.ppermute(own_stack, 'inner', [(i, (i + s) % group_width) for i in ran...  98.2 us
    all_to_all x1, waiting for transfers between devices, local(): lax.all_to_all(jnp.concatenate([send_q, send_kv], axis=3), 'inner', split...  18.1 us
    ppermute x7, starting transfers between devices, local(): lax.ppermute(own_stack, 'inner', [(i, (i + s) % group_width) for i in ran...  8.13 us
    ppermute x2, starting transfers between devices, shifted(): lax.ppermute(value, axis, [(source, source + steps) for source in range(l...  7.58 us
    ppermute x2, waiting for transfers between devices, shifted(): lax.ppermute(value, axis, [(source, source + steps) for source in range(l...  7.33 us
    unnamed x14, local copies, waits for them, and re-layouts  6.46 us
  transfers between devices with their start and end apart: 11, of which 9 were waited for; matrix products, arithmetic and copies ran while one was open for 3% of the time, Pallas kernels for 0%

profile of v1, /device:TPU:53, one launch (start us, length us, event | category | flops | bytes accessed | tf_op | source)
XLA Modules:
  0.0 281.6 jit_solution(11898446800073169266)
XLA Ops:
  0.0 0.0 copy-start
  0.0 0.0 copy-start.2
  0.0 0.8 add_select_fusion
  0.8 0.7 and_reduce_fusion.1
  1.6 0.3 convert_reduce_fusion
  1.8 0.8 select_reduce_fusion
  2.6 0.0 copy-done
  2.6 0.7 fusion
  3.3 1.4 fusion.1
  4.8 0.1 pad_maximum_fusion
  4.9 1.4 copy.25
  6.3 5.1 %all-to-all-start = ((bf16[8,1,128,768]{3,2,1,0:T(8,128)(2,1)}), bf16[8,1,128,768]{3,2,1,0:T(8,128)(2,1)S(1)}, u32[]{:S(2)}, u32[]{:S(2)}) async-start(bf16[8,1,128,768]{3,2,1,0:T(8,128)(2,1)} %copy.25), calls=%async_computation | async-start | bytes 3145728 | tf_op jit(solution)/shard_map/all_to_all | solution.py:58
  11.5 0.0 copy-done.3
  11.5 0.1 pad.5.clone
  11.6 0.0 copy-done.2
  11.6 0.2 and_reduce_fusion
  11.8 18.1 %all-to-all-done = bf16[8,1,128,768]{3,2,1,0:T(8,128)(2,1)S(1)} async-done(((bf16[8,1,128,768]{3,2,1,0:T(8,128)(2,1)}), bf16[8,1,128,768]{3,2,1,0:T(8,128)(2,1)S(1)}, u32[]{:S(2)}, u32[]{:S(2)}) %all-to-all-start) | async-done | bytes 1572896 | tf_op jit(solution)/shard_map/all_to_all | solution.py:58
  30.0 0.4 convolution_convert_fusion.3
  30.4 0.1 fusion.20
  30.6 2.9 %collective-permute-start = (bf16[528,256]{1,0:T(8,128)(2,1)S(1)}, bf16[528,256]{1,0:T(8,128)(2,1)S(1)}, u32[]{:S(2)}, u32[]{:S(2)}) collective-permute-start(bf16[528,256]{1,0:T(8,128)(2,1)S(1)} %get-tuple-element.18), channel_id=1, source_target_pairs={{0,16},{8,24},{16,32},{24,40},{32,48},{40,56},{48,64},{56,72},{64,... | collective-permute-start | bytes 811016 | tf_op jit(solution)/shard_map/ppermute | solution.py:14
  33.5 4.7 %collective-permute-start.1 = (bf16[528,256]{1,0:T(8,128)(2,1)S(1)}, bf16[528,256]{1,0:T(8,128)(2,1)S(1)}, u32[]{:S(2)}, u32[]{:S(2)}) collective-permute-start(bf16[528,256]{1,0:T(8,128)(2,1)S(1)} %get-tuple-element.18), channel_id=1, source_target_pairs={{0,32},{8,40},{16,48},{24,56},{32,64},{40,72},{48,80},{56,88},{64,... | collective-permute-start | bytes 811016 | tf_op jit(solution)/shard_map/ppermute | solution.py:14
  38.2 1.2 collective-permute-done
  39.4 6.1 %collective-permute-done.1 = bf16[528,256]{1,0:T(8,128)(2,1)S(1)} collective-permute-done((bf16[528,256]{1,0:T(8,128)(2,1)S(1)}, bf16[528,256]{1,0:T(8,128)(2,1)S(1)}, u32[]{:S(2)}, u32[]{:S(2)}) %collective-permute-start.1) | collective-permute-done | bytes 270368 | tf_op jit(solution)/shard_map/ppermute | solution.py:14
  45.5 1.0 pad_maximum_fusion.1
  46.5 1.7 collective-permute-start.2
  48.2 3.8 %collective-permute-start.3 = (bf16[3,528,256]{2,1,0:T(8,128)(2,1)}, bf16[3,528,256]{2,1,0:T(8,128)(2,1)}, u32[]{:S(2)}, u32[]{:S(2)}) collective-permute-start(bf16[3,528,256]{2,1,0:T(8,128)(2,1)} %pad_maximum_fusion.1), channel_id=1, source_target_pairs={{0,2},{1,3},{2,4},{3,5},{4,6},{5,7},{6,0},{7,1},{8,10},{9,11},{10,... | collective-permute-start | bytes 2433032 | tf_op jit(solution)/shard_map/ppermute | solution.py:92
  51.9 0.0 collective-permute-start.4
  51.9 0.0 collective-permute-start.5
  51.9 0.1 bitcast_dynamic-update-slice_fusion.7
  52.0 2.4 collective-permute-start.6
  54.4 23.7 %collective-permute-done.2 = bf16[3,528,256]{2,1,0:T(8,128)(2,1)} collective-permute-done((bf16[3,528,256]{2,1,0:T(8,128)(2,1)}, bf16[3,528,256]{2,1,0:T(8,128)(2,1)}, u32[]{:S(2)}, u32[]{:S(2)}) %collective-permute-start.2) | collective-permute-done | bytes 811040 | tf_op jit(solution)/shard_map/ppermute | solution.py:92
  78.1 0.0 collective-permute-start.7
  78.1 1.2 bitcast_dynamic-update-slice_fusion.6
  79.3 16.8 %collective-permute-done.3 = bf16[3,528,256]{2,1,0:T(8,128)(2,1)} collective-permute-done((bf16[3,528,256]{2,1,0:T(8,128)(2,1)}, bf16[3,528,256]{2,1,0:T(8,128)(2,1)}, u32[]{:S(2)}, u32[]{:S(2)}) %collective-permute-start.3) | collective-permute-done | bytes 811040 | tf_op jit(solution)/shard_map/ppermute | solution.py:92
  96.1 0.2 collective-permute-start.8
  96.3 1.2 bitcast_dynamic-update-slice_fusion.5
  97.5 22.4 %collective-permute-done.4 = bf16[3,528,256]{2,1,0:T(8,128)(2,1)} collective-permute-done((bf16[3,528,256]{2,1,0:T(8,128)(2,1)}, bf16[3,528,256]{2,1,0:T(8,128)(2,1)}, u32[]{:S(2)}, u32[]{:S(2)}) %collective-permute-start.4) | collective-permute-done | bytes 811040 | tf_op jit(solution)/shard_map/ppermute | solution.py:92
  119.9 1.2 bitcast_dynamic-update-slice_fusion.4
  121.1 35.2 %collective-permute-done.5 = bf16[3,528,256]{2,1,0:T(8,128)(2,1)S(1)} collective-permute-done((bf16[3,528,256]{2,1,0:T(8,128)(2,1)}, bf16[3,528,256]{2,1,0:T(8,128)(2,1)S(1)}, u32[]{:S(2)}, u32[]{:S(2)}) %collective-permute-start.5) | collective-permute-done | bytes 811040 | tf_op jit(solution)/shard_map/ppermute | solution.py:92
  156.3 0.1 bitcast_dynamic-update-slice_fusion.3
  156.4 0.0 collective-permute-done.6
  156.4 0.1 bitcast_dynamic-update-slice_fusion.2
  156.5 0.2 collective-permute-done.7
  156.6 0.1 bitcast_dynamic-update-slice_fusion.1
  156.7 0.0 collective-permute-done.8
  156.7 0.1 bitcast_dynamic-update-slice_fusion.first_ref
  156.8 0.0 copy-start.1
  156.8 2.7 copy-done.1
  159.5 2.4 constant_dynamic-slice_fusion
  161.9 2.5 collective-permute-start.9
  164.4 0.9 copy.30.qseg_ref
  165.2 0.6 fusion.22
  167.1 0.1 concatenate.19
  167.2 0.1 slice.69
  167.3 0.7 convolution_convert_fusion.1
  168.0 0.9 copy.29
  168.9 1.0 slice_reduce_fusion.7
  169.9 1.8 collective-permute-done.9.second_ref
  171.7 1.0 slice_reduce_fusion.5
  172.7 0.1 concatenate.22
  172.8 0.1 concatenate.23
  172.9 1.2 and_select_fusion.1
  174.1 0.6 concatenate.24.meta_ref
  174.7 106.9 %shard_map.55 = bf16[512,512]{1,0:T(8,128)(2,1)} custom-call(s32[81]{0:T(128)} %concatenate.24.meta_ref, bf16[512,512]{1,0:T(8,128)(2,1)} %bitcast.56, f32[512,1]{1,0:T(8,128)} %copy.30.qseg_ref, bf16[8,3,528,256]{3,2,1,0:T(8,128)(2,1)} %copy-done.1, bf16[8,2,528,256]{3,2,1,0:T(8,128)(2,1)} %collective-permute-done.9.second_ref), custom_call_target="tpu_custom_call" | custom-call | flops 21474836480 | bytes 11862016 | tf_op jit(solution)/shard_map/pallas_call | solution.py:224
  (13 shorter events, 0.2 us)
Async XLA Ops:
  0.0 2.6 copy-start
  0.0 11.6 %copy-start.2 = (s32[8,8]{1,0:T(8,128)S(1)}, s32[8,8]{1,0:T(8,128)}, u32[]{:S(2)}) copy-start(s32[8,8]{1,0:T(8,128)} %param.7) | copy-start | bytes 772
  0.0 11.5 %copy-start.3 = (s32[512]{0:T(512)S(1)}, s32[512]{0:T(512)}, u32[]{:S(2)}) copy-start(s32[512]{0:T(512)} %param.9) | copy-start | bytes 6148
  6.3 23.6 %all-to-all-start = ((bf16[8,1,128,768]{3,2,1,0:T(8,128)(2,1)}), bf16[8,1,128,768]{3,2,1,0:T(8,128)(2,1)S(1)}, u32[]{:S(2)}, u32[]{:S(2)}) async-start(bf16[8,1,128,768]{3,2,1,0:T(8,128)(2,1)} %copy.25), calls=%async_computation | async-start | bytes 3145728 | tf_op jit(solution)/shard_map/all_to_all | solution.py:58
  30.6 8.8 %collective-permute-start = (bf16[528,256]{1,0:T(8,128)(2,1)S(1)}, bf16[528,256]{1,0:T(8,128)(2,1)S(1)}, u32[]{:S(2)}, u32[]{:S(2)}) collective-permute-start(bf16[528,256]{1,0:T(8,128)(2,1)S(1)} %get-tuple-element.18), channel_id=1, source_target_pairs={{0,16},{8,24},{16,32},{24,40},{32,48},{40,56},{48,64},{56,72},{64,... | collective-permute-start | bytes 811016 | tf_op jit(solution)/shard_map/ppermute | solution.py:14
  33.5 12.0 %collective-permute-start.1 = (bf16[528,256]{1,0:T(8,128)(2,1)S(1)}, bf16[528,256]{1,0:T(8,128)(2,1)S(1)}, u32[]{:S(2)}, u32[]{:S(2)}) collective-permute-start(bf16[528,256]{1,0:T(8,128)(2,1)S(1)} %get-tuple-element.18), channel_id=1, source_target_pairs={{0,32},{8,40},{16,48},{24,56},{32,64},{40,72},{48,80},{56,88},{64,... | collective-permute-start | bytes 811016 | tf_op jit(solution)/shard_map/ppermute | solution.py:14
  46.5 31.6 %collective-permute-start.2 = (bf16[3,528,256]{2,1,0:T(8,128)(2,1)}, bf16[3,528,256]{2,1,0:T(8,128)(2,1)}, u32[]{:S(2)}, u32[]{:S(2)}) collective-permute-start(bf16[3,528,256]{2,1,0:T(8,128)(2,1)} %pad_maximum_fusion.1), channel_id=1, source_target_pairs={{0,1},{1,2},{2,3},{3,4},{4,5},{5,6},{6,7},{7,0},{8,9},{9,10},{10,1... | collective-permute-start | bytes 2433032 | tf_op jit(solution)/shard_map/ppermute | solution.py:92
  48.2 47.9 %collective-permute-start.3 = (bf16[3,528,256]{2,1,0:T(8,128)(2,1)}, bf16[3,528,256]{2,1,0:T(8,128)(2,1)}, u32[]{:S(2)}, u32[]{:S(2)}) collective-permute-start(bf16[3,528,256]{2,1,0:T(8,128)(2,1)} %pad_maximum_fusion.1), channel_id=1, source_target_pairs={{0,2},{1,3},{2,4},{3,5},{4,6},{5,7},{6,0},{7,1},{8,10},{9,11},{10,... | collective-permute-start | bytes 2433032 | tf_op jit(solution)/shard_map/ppermute | solution.py:92
  51.9 68.0 %collective-permute-start.4 = (bf16[3,528,256]{2,1,0:T(8,128)(2,1)}, bf16[3,528,256]{2,1,0:T(8,128)(2,1)}, u32[]{:S(2)}, u32[]{:S(2)}) collective-permute-start(bf16[3,528,256]{2,1,0:T(8,128)(2,1)} %pad_maximum_fusion.1), channel_id=1, source_target_pairs={{0,3},{1,4},{2,5},{3,6},{4,7},{5,0},{6,1},{7,2},{8,11},{9,12},{10,... | collective-permute-start | bytes 2433032 | tf_op jit(solution)/shard_map/ppermute | solution.py:92
  51.9 104.4 %collective-permute-start.5 = (bf16[3,528,256]{2,1,0:T(8,128)(2,1)}, bf16[3,528,256]{2,1,0:T(8,128)(2,1)S(1)}, u32[]{:S(2)}, u32[]{:S(2)}) collective-permute-start(bf16[3,528,256]{2,1,0:T(8,128)(2,1)} %pad_maximum_fusion.1), channel_id=1, source_target_pairs={{0,4},{1,5},{2,6},{3,7},{4,0},{5,1},{6,2},{7,3},{8,12},{9,13},{10,... | collective-permute-start | bytes 2433032 | tf_op jit(solution)/shard_map/ppermute | solution.py:92
  52.0 104.4 %collective-permute-start.6 = (bf16[3,528,256]{2,1,0:T(8,128)(2,1)}, bf16[3,528,256]{2,1,0:T(8,128)(2,1)S(1)}, u32[]{:S(2)}, u32[]{:S(2)}) collective-permute-start(bf16[3,528,256]{2,1,0:T(8,128)(2,1)} %pad_maximum_fusion.1), channel_id=1, source_target_pairs={{0,5},{1,6},{2,7},{3,0},{4,1},{5,2},{6,3},{7,4},{8,13},{9,14},{10,... | collective-permute-start | bytes 2433032 | tf_op jit(solution)/shard_map/ppermute | solution.py:92
  78.1 78.5 %collective-permute-start.7 = (bf16[3,528,256]{2,1,0:T(8,128)(2,1)}, bf16[3,528,256]{2,1,0:T(8,128)(2,1)S(1)}, u32[]{:S(2)}, u32[]{:S(2)}) collective-permute-start(bf16[3,528,256]{2,1,0:T(8,128)(2,1)} %pad_maximum_fusion.1), channel_id=1, source_target_pairs={{0,6},{1,7},{2,0},{3,1},{4,2},{5,3},{6,4},{7,5},{8,14},{9,15},{10,... | collective-permute-start | bytes 2433032 | tf_op jit(solution)/shard_map/ppermute | solution.py:92
  96.1 60.6 %collective-permute-start.8 = (bf16[3,528,256]{2,1,0:T(8,128)(2,1)}, bf16[3,528,256]{2,1,0:T(8,128)(2,1)S(1)}, u32[]{:S(2)}, u32[]{:S(2)}) collective-permute-start(bf16[3,528,256]{2,1,0:T(8,128)(2,1)} %pad_maximum_fusion.1), channel_id=1, source_target_pairs={{0,7},{1,0},{2,1},{3,2},{4,3},{5,4},{6,5},{7,6},{8,15},{9,8},{10,9... | collective-permute-start | bytes 2433032 | tf_op jit(solution)/shard_map/ppermute | solution.py:92
  156.8 2.7 copy-start.1
  161.9 9.8 %collective-permute-start.9 = (bf16[8,2,528,256]{3,2,1,0:T(8,128)(2,1)}, bf16[8,2,528,256]{3,2,1,0:T(8,128)(2,1)}, u32[]{:S(2)}, u32[]{:S(2)}) collective-permute-start(bf16[8,2,528,256]{3,2,1,0:T(8,128)(2,1)} %constant_dynamic-slice_fusion), channel_id=1, source_target_pairs={{0,8},{8,0},{16,24},{24,16},{32,40},{40,32},{48,56},{56,48},{64,72... | collective-permute-start | bytes 12976136 | tf_op jit(solution)/shard_map/ppermute | solution.py:101

commit v2 on v1

v2 whole, which is shorter than its diff:
```python
import math

import jax
import jax.numpy as jnp
from jax import lax
from jax.experimental import pallas as pl
from jax.experimental.pallas import tpu as pltpu
from jax.sharding import PartitionSpec as P


def shifted(value, axis, steps):
    count = lax.axis_size(axis)
    leading, last = (max(0, -steps), min(count, count - steps))
    return lax.ppermute(value, axis, [(source, source + steps) for source in range(leading, last)])


def select_rows(selector, blocks, pattern):
    return jnp.einsum(
        pattern, selector.astype(jnp.bfloat16), blocks, preferred_element_type=jnp.float32
    ).astype(jnp.bfloat16)


def local(q_load, kv_load, pack_dest, counts, segment_ids):
    group_width = lax.axis_size("inner")
    my_index = lax.axis_index("inner")
    capacity = pack_dest.shape[1]
    slot_count = capacity // 2
    pair_limit = -(-capacity // group_width)
    row_length = q_load.shape[0] // capacity
    query_width = q_load.shape[1]
    pair_width = kv_load.shape[1]
    head_size = pair_width // 2
    head_count = query_width // head_size
    slot_grid = lax.broadcasted_iota(jnp.int32, (group_width, capacity), 1)
    live_all = slot_grid < counts[:, None]
    owner_all = pack_dest // slot_count
    slot_numbers = jnp.arange(capacity, dtype=jnp.int32)
    earlier = slot_numbers[None, :] < slot_numbers[:, None]
    same_owner = owner_all[:, :, None] == owner_all[:, None, :]
    rank_all = jnp.sum(
        (earlier[None] & same_owner & live_all[:, None, :]).astype(jnp.int32), axis=2
    )
    shard_rows = jnp.arange(group_width, dtype=jnp.int32)
    mine_row = (shard_rows == my_index)[:, None]
    my_owner = jnp.sum(jnp.where(mine_row, owner_all, 0), axis=0)
    my_rank = jnp.sum(jnp.where(mine_row, rank_all, 0), axis=0)
    my_live = jnp.any(mine_row & live_all, axis=0)
    pair_ids = jnp.arange(pair_limit, dtype=jnp.int32)
    send_select = (
        my_live[None, None, :]
        & (my_owner[None, None, :] == shard_rows[:, None, None])
        & (my_rank[None, None, :] == pair_ids[None, :, None])
    )
    q_blocks = q_load.reshape(capacity, row_length, query_width)
    kv_blocks = kv_load.reshape(capacity, row_length, pair_width)
    send_q = select_rows(send_select, q_blocks, "jkc,crf->jkrf")
    send_kv = select_rows(send_select, kv_blocks, "jkc,crf->jkrf")
    recv_both = lax.all_to_all(
        jnp.concatenate([send_q, send_kv], axis=3), "inner", split_axis=0, concat_axis=0, tiled=True
    )
    recv_q = recv_both[..., :query_width]
    recv_kv = recv_both[..., query_width:]
    wanted = my_index * slot_count + jnp.arange(slot_count, dtype=jnp.int32)
    take_select = jnp.any(
        live_all[None, :, None, :]
        & (pack_dest[None, :, None, :] == wanted[:, None, None, None])
        & (rank_all[None, :, None, :] == pair_ids[None, None, :, None]),
        axis=3,
    )
    q_seq = select_rows(take_select, recv_q, "srk,rktf->stf").reshape(
        slot_count * row_length, query_width
    )
    kv_seq = select_rows(take_select, recv_kv, "srk,rktf->stf").reshape(
        slot_count * row_length, pair_width
    )
    tok_rows = q_seq.shape[0]
    owner_index = lax.axis_index(("outer", "inner"))
    outer_index = lax.axis_index("outer")
    score_scale = 1.0 / math.sqrt(head_size)
    extra_rows = 16
    seg_rows = tok_rows // pair_width
    seg_pad = jnp.zeros((extra_rows - seg_rows, pair_width), jnp.bfloat16)
    packed = jnp.concatenate(
        [kv_seq, segment_ids.astype(jnp.bfloat16).reshape(seg_rows, pair_width), seg_pad], axis=0
    )
    outer_reach = -(-(lax.axis_size("outer") * group_width // 4) // group_width)
    own_steps = list(range(0, outer_reach + 1, 2))
    partner_steps = list(range(1, outer_reach + 1, 2))
    moved = [packed if step == 0 else shifted(packed, "outer", step) for step in own_steps]
    own_stack = jnp.stack(moved)
    parity = outer_index % 2
    outer_count = lax.axis_size("outer")
    partner_pairs = [(o, o ^ 1) for o in range(outer_count)]
    first_seg = segment_ids[0].astype(jnp.bfloat16)
    last_seg = segment_ids[tok_rows - 1].astype(jnp.bfloat16)
    query_seg = segment_ids.astype(jnp.float32).reshape(tok_rows, 1)
    state = (
        jnp.full((head_count, tok_rows, head_size), -1e30, jnp.float32),
        jnp.zeros((head_count, tok_rows, head_size), jnp.float32),
        jnp.zeros((head_count, tok_rows, head_size), jnp.float32),
    )
    q_heads = jnp.transpose(q_seq.reshape(tok_rows, head_count, head_size), (1, 0, 2))

    def run(state, kv, key_device):
        key_first = kv[:, tok_rows, 0]
        key_last = kv[:, tok_rows + seg_rows - 1, pair_width - 1]
        needed = (
            (key_device >= 0)
            & (key_device <= owner_index)
            & (key_last >= first_seg)
            & (key_first <= last_seg)
        )
        whole = (
            (key_device < owner_index)
            & (key_first == key_last)
            & (key_first == first_seg)
            & (first_seg == last_seg)
        )
        needed = jnp.where(needed, jnp.where(whole, 1, 2), 0).astype(jnp.int32)
        meta = jnp.concatenate([owner_index.reshape(1).astype(jnp.int32), needed, key_device])
        return attend(meta, q_heads, query_seg, kv, state, score_scale)

    own_offsets = jnp.array(own_steps, jnp.int32)
    partner_offsets = jnp.array(partner_steps, jnp.int32)
    pieces = []
    states = []
    lag = 3
    for s in range(group_width):
        if s == 0:
            piece = own_stack
        else:
            source = own_stack
            if s > lag:
                source = lax.optimization_barrier((own_stack, states[s - lag]))[0]
            piece = lax.ppermute(
                source, "inner", [(i, (i + s) % group_width) for i in range(group_width)]
            )
        pieces.append(piece)
        inner_of = (my_index - s) % group_width
        state = run(state, piece, (outer_index - own_offsets) * group_width + inner_of)
        states.append(state[0])
    stacked = jnp.stack(pieces)
    offer = lax.dynamic_slice_in_dim(stacked, parity, len(partner_steps), axis=1)
    received = lax.ppermute(offer, "outer", partner_pairs)
    inner_all = (my_index - jnp.arange(group_width, dtype=jnp.int32)) % group_width
    received_device = (outer_index - partner_offsets[None, :]) * group_width + inner_all[:, None]
    state = run(
        state,
        received.reshape(-1, received.shape[2], pair_width),
        received_device.reshape(-1),
    )
    largest, denominator, weighted = state
    out = weighted / denominator
    return jnp.transpose(out, (1, 0, 2)).reshape(tok_rows, query_width).astype(jnp.bfloat16)


def attend(meta, q_heads, query_seg, blocks, state, score_scale):
    head_count, tok_rows, head_size = q_heads.shape
    block_count, packed_rows, pair_width = blocks.shape
    seg_rows = tok_rows // pair_width

    def kernel(meta_ref, q_ref, qseg_ref, kv_ref, m_in, l_in, acc_in, m_ref, l_ref, acc_ref):
        b = pl.program_id(0)

        @pl.when(b == 0)
        def _():
            m_ref[...] = m_in[...]
            l_ref[...] = l_in[...]
            acc_ref[...] = acc_in[...]

        def absorb(masked_block):
            keys = kv_ref[0, :tok_rows, :head_size]
            values = kv_ref[0, :tok_rows, head_size:]
            if masked_block:
                own = meta_ref[0]
                device = meta_ref[1 + block_count + b]
                seg_parts = [
                    kv_ref[0, tok_rows + r : tok_rows + r + 1, :].astype(jnp.float32)
                    for r in range(seg_rows)
                ]
                key_seg = jnp.concatenate(seg_parts, axis=1)
                key_pos = device * tok_rows + lax.broadcasted_iota(jnp.int32, (1, tok_rows), 1)
                query_pos = own * tok_rows + lax.broadcasted_iota(jnp.int32, (tok_rows, 1), 0)
                visible = (key_pos <= query_pos) & (key_seg == qseg_ref[...])

            def one_head(h, carry):
                scores = lax.dot_general(
                    q_ref[h], keys, (((1,), (1,)), ((), ())), preferred_element_type=jnp.float32
                )
                if masked_block:
                    scores = jnp.where(visible, scores, -1e30)
                m_prev = m_ref[h]
                m_next = jnp.maximum(m_prev, jnp.max(scores, axis=1, keepdims=True))
                factor = jnp.exp((m_prev - m_next) * score_scale)
                m_row = m_next[:, :1]
                if masked_block:
                    m_row = jnp.where(m_row == -1e30, 0.0, m_row)
                weights = jnp.exp((scores - m_row) * score_scale)
                l_ref[h] = l_ref[h] * factor + jnp.sum(weights, axis=1, keepdims=True)
                acc_ref[h] = acc_ref[h] * factor + jnp.dot(
                    weights.astype(jnp.bfloat16), values, preferred_element_type=jnp.float32
                )
                m_ref[h] = m_next
                return carry

            lax.fori_loop(0, head_count, one_head, 0)

        mode = meta_ref[1 + b]
        for masked_block, code in ((False, 1), (True, 2)):
            @pl.when(mode == code)
            def _(masked_block=masked_block):
                absorb(masked_block)

    state_spec = pl.BlockSpec(state[0].shape, lambda b, meta: (0, 0, 0))
    grid_spec = pltpu.PrefetchScalarGridSpec(
        num_scalar_prefetch=1,
        grid=(block_count,),
        in_specs=[
            pl.BlockSpec(q_heads.shape, lambda b, meta: (0, 0, 0)),
            pl.BlockSpec(query_seg.shape, lambda b, meta: (0, 0)),
            pl.BlockSpec((1, packed_rows, pair_width), lambda b, meta: (b, 0, 0)),
            state_spec,
            state_spec,
            state_spec,
        ],
        out_specs=[state_spec, state_spec, state_spec],
    )
    flops = 4 * block_count * tok_rows * tok_rows * head_size * head_count
    state_shape = jax.ShapeDtypeStruct(state[0].shape, jnp.float32)
    return pl.pallas_call(
        kernel,
        grid_spec=grid_spec,
        out_shape=[state_shape, state_shape, state_shape],
        input_output_aliases={4: 0, 5: 1, 6: 2},
        compiler_params=pltpu.CompilerParams(dimension_semantics=("arbitrary",)),
        cost_estimate=pl.CostEstimate(
            flops=flops,
            transcendentals=block_count * tok_rows * tok_rows * head_count,
            bytes_accessed=blocks.size * 2 + q_heads.size * 2 + state[0].size * 24,
        ),
    )(meta, q_heads, query_seg, blocks, *state)


def solution(mesh):
    in_specs = (
        P(("outer", "inner"), None),
        P(("outer", "inner"), None),
        P("outer", None),
        P("outer"),
        P(("outer", "inner")),
    )
    out_specs = P(("outer", "inner"), None)
    return jax.shard_map(local, mesh=mesh, in_specs=in_specs, out_specs=out_specs, check_vma=False)
```

time: 280 us -> 297 us (1.061)
  the two profiles are of different devices: /device:TPU:53 before, /device:TPU:67 now
where the time goes in v2:
time: 297 us; the launch traced here: 294 us
  Pallas kernels  161 us (54%)
  waiting for transfers between devices  48.4 us (16%)
  other arithmetic  32.1 us (11%)
  starting transfers between devices  24 us (8%)
  local copies, waits for them, and re-layouts  23.6 us (8%)
  matrix products  3.28 us (1%)
    pallas_call x9, Pallas kernels, attend(): pl.pallas_call(kernel, grid_spec=grid_spec, out_shape=[state_shape, state...  161 us
    all_to_all x1, waiting for transfers between devices, local(): lax.all_to_all(jnp.concatenate([send_q, send_kv], axis=3), 'inner', split...  20.6 us
    eq x9, other arithmetic, run(): key_first == key_last  19 us
    ppermute x7, waiting for transfers between devices, local(): lax.ppermute(source, 'inner', [(i, (i + s) % group_width) for i in range(...  18.5 us
    ppermute x7, starting transfers between devices, local(): lax.ppermute(source, 'inner', [(i, (i + s) % group_width) for i in range(...  11.5 us
    unnamed x24, local copies, waits for them, and re-layouts  9.29 us
    ppermute x2, waiting for transfers between devices, shifted(): lax.ppermute(value, axis, [(source, source + steps) for source in range(l...  9.25 us
    ppermute x2, starting transfers between devices, shifted(): lax.ppermute(value, axis, [(source, source + steps) for source in range(l...  7.12 us
  transfers between devices with their start and end apart: 11, of which 5 were waited for; matrix products, arithmetic and copies ran while one was open for 13% of the time, Pallas kernels for 33%

profile of v2, /device:TPU:67, one launch (start us, length us, event | category | flops | bytes accessed | tf_op | source)
XLA Modules:
  0.0 294.1 jit_solution(3478401471582831396)
XLA Ops:
  0.0 0.8 add_select_fusion
  0.8 0.7 and_reduce_fusion.1
  1.8 0.8 select_reduce_fusion
  2.6 1.4 fusion.1
  4.1 0.7 fusion
  4.9 1.4 copy.75
  6.3 5.3 %all-to-all-start = ((bf16[8,1,128,768]{3,2,1,0:T(8,128)(2,1)}), bf16[8,1,128,768]{3,2,1,0:T(8,128)(2,1)S(1)}, u32[]{:S(2)}, u32[]{:S(2)}) async-start(bf16[8,1,128,768]{3,2,1,0:T(8,128)(2,1)} %copy.75), calls=%async_computation | async-start | bytes 3145728 | tf_op jit(solution)/shard_map/all_to_all | solution.py:58
  12.0 20.6 %all-to-all-done = bf16[8,1,128,768]{3,2,1,0:T(8,128)(2,1)S(1)} async-done(((bf16[8,1,128,768]{3,2,1,0:T(8,128)(2,1)}), bf16[8,1,128,768]{3,2,1,0:T(8,128)(2,1)S(1)}, u32[]{:S(2)}, u32[]{:S(2)}) %all-to-all-start) | async-done | bytes 1572896 | tf_op jit(solution)/shard_map/all_to_all | solution.py:58
  33.1 0.8 fusion.21
  34.0 4.8 %collective-permute-start.1 = (bf16[528,256]{1,0:T(8,128)(2,1)}, bf16[528,256]{1,0:T(8,128)(2,1)S(1)}, u32[]{:S(2)}, u32[]{:S(2)}) collective-permute-start(bf16[528,256]{1,0:T(8,128)(2,1)} %get-tuple-element.120), channel_id=1, source_target_pairs={{0,32},{8,40},{16,48},{24,56},{32,64},{40,72},{48,80},{56,88},{64,... | collective-permute-start | bytes 811016 | tf_op jit(solution)/shard_map/ppermute | solution.py:14
  38.8 2.3 collective-permute-start
  41.2 0.8 copy.82.qseg_ref
  42.0 0.6 fusion.23
  44.1 2.2 collective-permute-done.1
  46.3 7.0 %collective-permute-done = bf16[528,256]{1,0:T(8,128)(2,1)S(1)} collective-permute-done((bf16[528,256]{1,0:T(8,128)(2,1)}, bf16[528,256]{1,0:T(8,128)(2,1)S(1)}, u32[]{:S(2)}, u32[]{:S(2)}) %collective-permute-start) | collective-permute-done | bytes 270368 | tf_op jit(solution)/shard_map/ppermute | solution.py:14
  53.3 1.0 pad_maximum_fusion.1.kv_ref
  54.3 0.7 convolution_convert_fusion.1
  55.3 0.9 copy.103
  56.2 0.5 collective-permute-start.3
  56.7 4.5 %collective-permute-start.4 = (bf16[3,528,256]{2,1,0:T(8,128)(2,1)}, bf16[3,528,256]{2,1,0:T(8,128)(2,1)}, u32[]{:S(2)}, u32[]{:S(2)}) collective-permute-start(bf16[3,528,256]{2,1,0:T(8,128)(2,1)} %pad_maximum_fusion.1.kv_ref), channel_id=1, source_target_pairs={{0,3},{1,4},{2,5},{3,6},{4,7},{5,0},{6,1},{7,2},{8,11},{9,12},{10,... | collective-permute-start | bytes 2433032 | tf_op jit(solution)/shard_map/ppermute | solution.py:135
  61.2 2.3 compare_reduce_fusion.29
  63.5 0.9 bitcast_dynamic-update-slice_fusion.7
  64.5 0.6 pad_add_fusion.1.meta_ref
  65.1 1.0 broadcast_in_dim.80.m_in
  66.1 1.1 broadcast_12_l_in_acc_in.2.l_in
  67.2 1.1 broadcast_12_l_in_acc_in.2.clone.acc_in
  68.3 12.2 %shard_map.73 = (f32[4,512,128]{2,1,0:T(8,128)}, f32[4,512,128]{2,1,0:T(8,128)}, f32[4,512,128]{2,1,0:T(8,128)}) custom-call(s32[7]{0:T(128)} %pad_add_fusion.1.meta_ref, bf16[4,512,128]{2,1,0:T(8,128)(2,1)} %bitcast.63, f32[512,1]{1,0:T(8,128)} %copy.82.qseg_ref, ...), custom_call_target="tpu_custom_call", output_to_operand_aliasing={{0}: (4, {}), {1}: (5, {}), {2}: (6, {})} | custom-call | flops 1610612736 | bytes 7626752 | tf_op jit(solution)/shard_map/pallas_call | solution.py:230
  80.5 5.7 %collective-permute-done.2.kv_ref = bf16[3,528,256]{2,1,0:T(8,128)(2,1)} collective-permute-done((bf16[3,528,256]{2,1,0:T(8,128)(2,1)}, bf16[3,528,256]{2,1,0:T(8,128)(2,1)}, u32[]{:S(2)}, u32[]{:S(2)}) %collective-permute-start.2) | collective-permute-done | bytes 811040 | tf_op jit(solution)/shard_map/ppermute | solution.py:135
  86.2 2.3 compare_reduce_fusion.33
  88.5 0.6 pad_add_fusion.meta_ref
  89.1 12.2 %shard_map.74 = (f32[4,512,128]{2,1,0:T(8,128)}, f32[4,512,128]{2,1,0:T(8,128)}, f32[4,512,128]{2,1,0:T(8,128)}) custom-call(s32[7]{0:T(128)} %pad_add_fusion.meta_ref, bf16[4,512,128]{2,1,0:T(8,128)(2,1)} %bitcast.64, f32[512,1]{1,0:T(8,128)} %copy.82.qseg_ref, ...), custom_call_target="tpu_custom_call", output_to_operand_aliasing={{0}: (4, {}), {1}: (5, {}), {2}: (6, {})} | custom-call | flops 1610612736 | bytes 7626752 | tf_op jit(solution)/shard_map/pallas_call | solution.py:230
  101.3 1.6 compare_reduce_fusion.25
  102.9 0.6 pad_add_fusion.2.meta_ref
  103.5 12.2 %shard_map.75 = (f32[4,512,128]{2,1,0:T(8,128)}, f32[4,512,128]{2,1,0:T(8,128)}, f32[4,512,128]{2,1,0:T(8,128)}) custom-call(s32[7]{0:T(128)} %pad_add_fusion.2.meta_ref, bf16[4,512,128]{2,1,0:T(8,128)(2,1)} %bitcast.65, f32[512,1]{1,0:T(8,128)} %copy.82.qseg_ref, ...), custom_call_target="tpu_custom_call", output_to_operand_aliasing={{0}: (4, {}), {1}: (5, {}), {2}: (6, {})} | custom-call | flops 1610612736 | bytes 7626752 | tf_op jit(solution)/shard_map/pallas_call | solution.py:230
  115.7 2.4 compare_reduce_fusion.21
  118.1 0.6 pad_add_fusion.3.meta_ref
  118.7 12.2 %shard_map.76 = (f32[4,512,128]{2,1,0:T(8,128)}, f32[4,512,128]{2,1,0:T(8,128)}, f32[4,512,128]{2,1,0:T(8,128)}) custom-call(s32[7]{0:T(128)} %pad_add_fusion.3.meta_ref, bf16[4,512,128]{2,1,0:T(8,128)(2,1)} %bitcast.66, f32[512,1]{1,0:T(8,128)} %copy.82.qseg_ref, ...), custom_call_target="tpu_custom_call", output_to_operand_aliasing={{0}: (4, {}), {1}: (5, {}), {2}: (6, {})} | custom-call | flops 1610612736 | bytes 7626752 | tf_op jit(solution)/shard_map/pallas_call | solution.py:230
  130.9 6.5 %collective-permute-start.7 = (bf16[3,528,256]{2,1,0:T(8,128)(2,1)}, bf16[3,528,256]{2,1,0:T(8,128)(2,1)S(1)}, u32[]{:S(2)}, u32[]{:S(2)}) collective-permute-start(bf16[3,528,256]{2,1,0:T(8,128)(2,1)} %pad_maximum_fusion.1.kv_ref), channel_id=1, source_target_pairs={{0,6},{1,7},{2,0},{3,1},{4,2},{5,3},{6,4},{7,5},{8,14},{9,15},{10,... | collective-permute-start | bytes 2433032 | tf_op jit(solution)/shard_map/ppermute | solution.py:135
  137.4 2.1 bitcast_dynamic-update-slice_fusion.6
  139.5 1.0 bitcast_dynamic-update-slice_fusion.5
  140.4 2.3 compare_reduce_fusion.17
  142.8 0.6 pad_add_fusion.4.meta_ref
  143.4 12.2 %shard_map.77 = (f32[4,512,128]{2,1,0:T(8,128)}, f32[4,512,128]{2,1,0:T(8,128)}, f32[4,512,128]{2,1,0:T(8,128)}) custom-call(s32[7]{0:T(128)} %pad_add_fusion.4.meta_ref, bf16[4,512,128]{2,1,0:T(8,128)(2,1)} %bitcast.67, f32[512,1]{1,0:T(8,128)} %copy.82.qseg_ref, ...), custom_call_target="tpu_custom_call", output_to_operand_aliasing={{0}: (4, {}), {1}: (5, {}), {2}: (6, {})} | custom-call | flops 1610612736 | bytes 7626752 | tf_op jit(solution)/shard_map/pallas_call | solution.py:230
  155.6 2.1 bitcast_dynamic-update-slice_fusion.4
  157.7 2.1 bitcast_dynamic-update-slice_fusion.3
  159.8 1.0 bitcast_dynamic-update-slice_fusion.2
  160.7 1.1 bitcast_dynamic-update-slice_fusion.1
  161.8 12.8 %collective-permute-done.8.kv_ref = bf16[3,528,256]{2,1,0:T(8,128)(2,1)S(1)} collective-permute-done((bf16[3,528,256]{2,1,0:T(8,128)(2,1)}, bf16[3,528,256]{2,1,0:T(8,128)(2,1)S(1)}, u32[]{:S(2)}, u32[]{:S(2)}) %collective-permute-start.8) | collective-permute-done | bytes 811040 | tf_op jit(solution)/shard_map/ppermute | solution.py:135
  174.6 1.0 bitcast_dynamic-update-slice_fusion
  175.6 4.6 %constant_dynamic-slice_fusion = bf16[8,2,528,256]{3,2,1,0:T(8,128)(2,1)} fusion(bf16[8,3,528,256]{3,2,1,0:T(8,128)(2,1)} %bitcast_dynamic-update-slice_fusion, s32[]{:T(128)S(6)} %select_n.142), kind=kLoop, calls=%fused_computation.132 | loop fusion | bytes 8650756 | tf_op jit(solution)/shard_map/dynamic_slice | solution.py:143
  180.4 1.6 compare_reduce_fusion.5
  182.0 1.6 compare_reduce_fusion.9
  183.6 0.6 pad_add_fusion.7.meta_ref
  184.2 0.6 pad_add_fusion.8.meta_ref
  184.8 12.2 %shard_map.78 = (f32[4,512,128]{2,1,0:T(8,128)}, f32[4,512,128]{2,1,0:T(8,128)}, f32[4,512,128]{2,1,0:T(8,128)}) custom-call(s32[7]{0:T(128)} %pad_add_fusion.8.meta_ref, bf16[4,512,128]{2,1,0:T(8,128)(2,1)} %bitcast.68, f32[512,1]{1,0:T(8,128)} %copy.82.qseg_ref, ...), custom_call_target="tpu_custom_call", output_to_operand_aliasing={{0}: (4, {}), {1}: (5, {}), {2}: (6, {})} | custom-call | flops 1610612736 | bytes 7626752 | tf_op jit(solution)/shard_map/pallas_call | solution.py:230
  197.0 12.2 %shard_map.79 = (f32[4,512,128]{2,1,0:T(8,128)}, f32[4,512,128]{2,1,0:T(8,128)}, f32[4,512,128]{2,1,0:T(8,128)}) custom-call(s32[7]{0:T(128)} %pad_add_fusion.7.meta_ref, bf16[4,512,128]{2,1,0:T(8,128)(2,1)} %bitcast.69, f32[512,1]{1,0:T(8,128)} %copy.82.qseg_ref, ...), custom_call_target="tpu_custom_call", output_to_operand_aliasing={{0}: (4, {}), {1}: (5, {}), {2}: (6, {})} | custom-call | flops 1610612736 | bytes 7626752 | tf_op jit(solution)/shard_map/pallas_call | solution.py:230
  209.2 1.6 compare_reduce_fusion.13
  210.8 0.7 pad_add_fusion.6.meta_ref
  211.5 12.2 %shard_map.80 = (f32[4,512,128]{2,1,0:T(8,128)}, f32[4,512,128]{2,1,0:T(8,128)}, f32[4,512,128]{2,1,0:T(8,128)}) custom-call(s32[7]{0:T(128)} %pad_add_fusion.6.meta_ref, bf16[4,512,128]{2,1,0:T(8,128)(2,1)} %bitcast.70, f32[512,1]{1,0:T(8,128)} %copy.82.qseg_ref, ...), custom_call_target="tpu_custom_call", output_to_operand_aliasing={{0}: (4, {}), {1}: (5, {}), {2}: (6, {})} | custom-call | flops 1610612736 | bytes 7626752 | tf_op jit(solution)/shard_map/pallas_call | solution.py:230
  223.7 3.3 %compare_reduce_fusion.1 = (pred[16]{0:T(512)(128)(4,1)S(1)}, pred[16]{0:T(512)(128)(4,1)S(1)}, pred[16]{0:T(512)(128)(4,1)S(1)}, pred[16]{0:T(512)(128)(4,1)S(1)}) fusion(bf16[16,528,256]{2,1,0:T(8,128)(2,1)} %bitcast.27.kv_ref, bf16[]{:T(256)} %bitcast.18, bf16[]{:T(256)} %bitcast.19), kind=kLoop, calls=%fused_computation.26 | loop fusion | flops 64 | bytes 132 | tf_op jit(solution)/shard_map/eq | solution.py:115
  227.0 0.6 pad_add_fusion.5.meta_ref
  227.6 63.5 %shard_map.81 = (f32[4,512,128]{2,1,0:T(8,128)}, f32[4,512,128]{2,1,0:T(8,128)}, f32[4,512,128]{2,1,0:T(8,128)}) custom-call(s32[33]{0:T(128)} %pad_add_fusion.5.meta_ref, bf16[4,512,128]{2,1,0:T(8,128)(2,1)} %bitcast.71, f32[512,1]{1,0:T(8,128)} %copy.82.qseg_ref, ...), custom_call_target="tpu_custom_call", output_to_operand_aliasing={{0}: (4, {}), {1}: (5, {}), {2}: (6, {})} | custom-call | flops 8589934592 | bytes 11141120 | tf_op jit(solution)/shard_map/pallas_call | solution.py:230
  291.2 1.7 fusion.4
  293.1 1.0 copy.91
  (60 shorter events, 2.1 us)
Async XLA Ops:
  0.0 4.1 %copy-start = (bf16[1024,512]{1,0:T(8,128)(2,1)S(1)}, bf16[1024,512]{1,0:T(8,128)(2,1)}, u32[]{:S(2)}) copy-start(bf16[1024,512]{1,0:T(8,128)(2,1)} %param.7) | copy-start | bytes 3145732
  0.0 11.8 %copy-start.6 = (s32[8,8]{1,0:T(8,128)S(1)}, s32[8,8]{1,0:T(8,128)}, u32[]{:S(2)}) copy-start(s32[8,8]{1,0:T(8,128)} %param.9) | copy-start | bytes 772
  0.0 11.7 %copy-start.7 = (s32[512]{0:T(512)S(1)}, s32[512]{0:T(512)}, u32[]{:S(2)}) copy-start(s32[512]{0:T(512)} %param.11) | copy-start | bytes 6148
  6.3 26.3 %all-to-all-start = ((bf16[8,1,128,768]{3,2,1,0:T(8,128)(2,1)}), bf16[8,1,128,768]{3,2,1,0:T(8,128)(2,1)S(1)}, u32[]{:S(2)}, u32[]{:S(2)}) async-start(bf16[8,1,128,768]{3,2,1,0:T(8,128)(2,1)} %copy.75), calls=%async_computation | async-start | bytes 3145728 | tf_op jit(solution)/shard_map/all_to_all | solution.py:58
  34.0 12.3 %collective-permute-start.1 = (bf16[528,256]{1,0:T(8,128)(2,1)}, bf16[528,256]{1,0:T(8,128)(2,1)S(1)}, u32[]{:S(2)}, u32[]{:S(2)}) collective-permute-start(bf16[528,256]{1,0:T(8,128)(2,1)} %get-tuple-element.120), channel_id=1, source_target_pairs={{0,32},{8,40},{16,48},{24,56},{32,64},{40,72},{48,80},{56,88},{64,... | collective-permute-start | bytes 811016 | tf_op jit(solution)/shard_map/ppermute | solution.py:14
  38.8 14.5 %collective-permute-start = (bf16[528,256]{1,0:T(8,128)(2,1)}, bf16[528,256]{1,0:T(8,128)(2,1)S(1)}, u32[]{:S(2)}, u32[]{:S(2)}) collective-permute-start(bf16[528,256]{1,0:T(8,128)(2,1)} %get-tuple-element.120), channel_id=1, source_target_pairs={{0,16},{8,24},{16,32},{24,40},{32,48},{40,56},{48,64},{56,72},{64,... | collective-permute-start | bytes 811016 | tf_op jit(solution)/shard_map/ppermute | solution.py:14
  54.3 31.9 %collective-permute-start.2 = (bf16[3,528,256]{2,1,0:T(8,128)(2,1)}, bf16[3,528,256]{2,1,0:T(8,128)(2,1)}, u32[]{:S(2)}, u32[]{:S(2)}) collective-permute-start(bf16[3,528,256]{2,1,0:T(8,128)(2,1)} %pad_maximum_fusion.1.kv_ref), channel_id=1, source_target_pairs={{0,1},{1,2},{2,3},{3,4},{4,5},{5,6},{6,7},{7,0},{8,9},{9,10},{10,1... | collective-permute-start | bytes 2433032 | tf_op jit(solution)/shard_map/ppermute | solution.py:135
  56.2 45.2 %collective-permute-start.3 = (bf16[3,528,256]{2,1,0:T(8,128)(2,1)}, bf16[3,528,256]{2,1,0:T(8,128)(2,1)S(1)}, u32[]{:S(2)}, u32[]{:S(2)}) collective-permute-start(bf16[3,528,256]{2,1,0:T(8,128)(2,1)} %pad_maximum_fusion.1.kv_ref), channel_id=1, source_target_pairs={{0,2},{1,3},{2,4},{3,5},{4,6},{5,7},{6,0},{7,1},{8,10},{9,11},{10,... | collective-permute-start | bytes 2433032 | tf_op jit(solution)/shard_map/ppermute | solution.py:135
  56.7 59.0 %collective-permute-start.4 = (bf16[3,528,256]{2,1,0:T(8,128)(2,1)}, bf16[3,528,256]{2,1,0:T(8,128)(2,1)}, u32[]{:S(2)}, u32[]{:S(2)}) collective-permute-start(bf16[3,528,256]{2,1,0:T(8,128)(2,1)} %pad_maximum_fusion.1.kv_ref), channel_id=1, source_target_pairs={{0,3},{1,4},{2,5},{3,6},{4,7},{5,0},{6,1},{7,2},{8,11},{9,12},{10,... | collective-permute-start | bytes 2433032 | tf_op jit(solution)/shard_map/ppermute | solution.py:135
  101.3 39.1 %collective-permute-start.5 = (bf16[3,528,256]{2,1,0:T(8,128)(2,1)}, bf16[3,528,256]{2,1,0:T(8,128)(2,1)}, u32[]{:S(2)}, u32[]{:S(2)}) collective-permute-start(bf16[3,528,256]{2,1,0:T(8,128)(2,1)} %pad_maximum_fusion.1.kv_ref), channel_id=1, source_target_pairs={{0,4},{1,5},{2,6},{3,7},{4,0},{5,1},{6,2},{7,3},{8,12},{9,13},{10,... | collective-permute-start | bytes 2433032 | tf_op jit(solution)/shard_map/ppermute | solution.py:135
  101.3 2.2 copy-start.4
  115.7 23.7 %copy-start.5 = (bf16[3,528,256]{2,1,0:T(8,128)(2,1)S(1)}, bf16[3,528,256]{2,1,0:T(8,128)(2,1)}, u32[]{:S(2)}) copy-start(bf16[3,528,256]{2,1,0:T(8,128)(2,1)} %copy-done.4) | copy-start | bytes 2433028
  115.7 44.0 %collective-permute-start.6 = (bf16[3,528,256]{2,1,0:T(8,128)(2,1)}, bf16[3,528,256]{2,1,0:T(8,128)(2,1)S(1)}, u32[]{:S(2)}, u32[]{:S(2)}) collective-permute-start(bf16[3,528,256]{2,1,0:T(8,128)(2,1)} %pad_maximum_fusion.1.kv_ref), channel_id=1, source_target_pairs={{0,5},{1,6},{2,7},{3,0},{4,1},{5,2},{6,3},{7,4},{8,13},{9,14},{10,... | collective-permute-start | bytes 2433032 | tf_op jit(solution)/shard_map/ppermute | solution.py:135
  130.9 29.8 %collective-permute-start.7 = (bf16[3,528,256]{2,1,0:T(8,128)(2,1)}, bf16[3,528,256]{2,1,0:T(8,128)(2,1)S(1)}, u32[]{:S(2)}, u32[]{:S(2)}) collective-permute-start(bf16[3,528,256]{2,1,0:T(8,128)(2,1)} %pad_maximum_fusion.1.kv_ref), channel_id=1, source_target_pairs={{0,6},{1,7},{2,0},{3,1},{4,2},{5,3},{6,4},{7,5},{8,14},{9,15},{10,... | collective-permute-start | bytes 2433032 | tf_op jit(solution)/shard_map/ppermute | solution.py:135
  155.6 19.0 %collective-permute-start.8 = (bf16[3,528,256]{2,1,0:T(8,128)(2,1)}, bf16[3,528,256]{2,1,0:T(8,128)(2,1)S(1)}, u32[]{:S(2)}, u32[]{:S(2)}) collective-permute-start(bf16[3,528,256]{2,1,0:T(8,128)(2,1)} %pad_maximum_fusion.1.kv_ref), channel_id=1, source_target_pairs={{0,7},{1,0},{2,1},{3,2},{4,3},{5,4},{6,5},{7,6},{8,15},{9,8},{10,9... | collective-permute-start | bytes 2433032 | tf_op jit(solution)/shard_map/ppermute | solution.py:135
  159.8 20.5 %copy-start.8 = (s32[2]{0:T(128)S(1)}, s32[2]{0:T(128)}, u32[]{:S(2)}) copy-start(s32[2]{0:T(128)} %constant.124) | copy-start | bytes 28
  159.8 20.6 %copy-start.1 = (bf16[3,528,256]{2,1,0:T(8,128)(2,1)}, bf16[3,528,256]{2,1,0:T(8,128)(2,1)S(1)}, u32[]{:S(2)}) copy-start(bf16[3,528,256]{2,1,0:T(8,128)(2,1)S(1)} %collective-permute-done.6.kv_ref) | copy-start | bytes 2433028
  160.7 36.3 %copy-start.2 = (bf16[3,528,256]{2,1,0:T(8,128)(2,1)}, bf16[3,528,256]{2,1,0:T(8,128)(2,1)S(1)}, u32[]{:S(2)}) copy-start(bf16[3,528,256]{2,1,0:T(8,128)(2,1)S(1)} %collective-permute-done.7.kv_ref) | copy-start | bytes 2433028
  174.6 34.6 %copy-start.3 = (bf16[3,528,256]{2,1,0:T(8,128)(2,1)}, bf16[3,528,256]{2,1,0:T(8,128)(2,1)S(1)}, u32[]{:S(2)}) copy-start(bf16[3,528,256]{2,1,0:T(8,128)(2,1)S(1)} %collective-permute-done.8.kv_ref) | copy-start | bytes 2433028
  180.2 43.5 %collective-permute-start.9 = (bf16[8,2,528,256]{3,2,1,0:T(8,128)(2,1)}, bf16[8,2,528,256]{3,2,1,0:T(8,128)(2,1)}, u32[]{:S(2)}, u32[]{:S(2)}) collective-permute-start(bf16[8,2,528,256]{3,2,1,0:T(8,128)(2,1)} %constant_dynamic-slice_fusion), channel_id=1, source_target_pairs={{0,8},{8,0},{16,24},{24,16},{32,40},{40,32},{48,56},{56,48},{64,72... | collective-permute-start | bytes 12976136 | tf_op jit(solution)/shard_map/ppermute | solution.py:144

commit v3 on v1

--- a/solution.py
+++ b/solution.py
@@ -88,12 +88,15 @@
     partner_steps = list(range(1, outer_reach + 1, 2))
     moved = [packed if step == 0 else shifted(packed, "outer", step) for step in own_steps]
     own_stack = jnp.stack(moved)
-    inner_shifts = [own_stack] + [
-        lax.ppermute(own_stack, "inner", [(i, (i + s) % group_width) for i in range(group_width)])
-        for s in range(1, group_width)
+    pair_mate = lax.ppermute(own_stack, "inner", [(i, i ^ 1) for i in range(group_width)])
+    pair = jnp.stack([own_stack, pair_mate])
+    pair_shifts = [pair] + [
+        lax.ppermute(pair, "inner", [(i, (i + 2 * t) % group_width) for i in range(group_width)])
+        for t in range(1, group_width // 2)
     ]
-    gathered = jnp.stack(inner_shifts)
-    inner_of = (my_index - jnp.arange(group_width, dtype=jnp.int32)) % group_width
+    gathered = jnp.concatenate(pair_shifts)
+    entry = jnp.arange(group_width, dtype=jnp.int32)
+    inner_of = ((my_index - 2 * (entry // 2)) % group_width) ^ (entry % 2)
     parity = outer_index % 2
     offer = lax.dynamic_slice_in_dim(gathered, parity, len(partner_steps), axis=1)
     outer_count = lax.axis_size("outer")

time: 280 us -> 261 us (0.932)
  the two profiles are of different devices: /device:TPU:53 before, /device:TPU:67 now
where the time goes in v3:
time: 261 us; the launch traced here: 263 us
  waiting for transfers between devices  119 us (46%)
  Pallas kernels  99.8 us (38%)
  starting transfers between devices  16.9 us (6%)
  local copies, waits for them, and re-layouts  15.6 us (6%)
  other arithmetic  6.95 us (3%)
  matrix products  3.28 us (1%)
    pallas_call x1, Pallas kernels, attend(): pl.pallas_call(kernel, grid_spec=grid_spec, out_shape=jax.ShapeDtypeStruc...  99.8 us
    ppermute x3, waiting for transfers between devices, local(): lax.ppermute(pair, 'inner', [(i, (i + 2 * t) % group_width) for i in rang...  66.7 us
    all_to_all x1, waiting for transfers between devices, local(): lax.all_to_all(jnp.concatenate([send_q, send_kv], axis=3), 'inner', split...  20.6 us
    ppermute x1, waiting for transfers between devices, local(): lax.ppermute(own_stack, 'inner', [(i, i ^ 1) for i in range(group_width)])  17.8 us
    ppermute x2, waiting for transfers between devices, shifted(): lax.ppermute(value, axis, [(source, source + steps) for source in range(l...  12.1 us
    ppermute x2, starting transfers between devices, shifted(): lax.ppermute(value, axis, [(source, source + steps) for source in range(l...  7.13 us
    all_to_all x1, starting transfers between devices, local(): lax.all_to_all(jnp.concatenate([send_q, send_kv], axis=3), 'inner', split...  5.33 us
  transfers between devices with their start and end apart: 8, of which 8 were waited for; matrix products, arithmetic and copies ran while one was open for 3% of the time, Pallas kernels for 0%

profile of v3, /device:TPU:67, one launch (start us, length us, event | category | flops | bytes accessed | tf_op | source)
XLA Modules:
  0.0 262.9 jit_solution(1589041059796308278)
XLA Ops:
  0.0 0.0 copy-start
  0.0 0.8 add_select_fusion
  0.8 0.7 and_reduce_fusion.1
  1.5 0.3 convert_reduce_fusion
  1.8 0.8 select_reduce_fusion
  2.6 1.4 fusion.1
  4.0 0.0 copy-done
  4.1 0.7 fusion
  4.8 0.1 pad_maximum_fusion.1
  4.9 0.0 copy-start.6
  4.9 0.0 copy-start.5
  4.9 1.4 copy.25
  6.3 5.3 %all-to-all-start = ((bf16[8,1,128,768]{3,2,1,0:T(8,128)(2,1)}), bf16[8,1,128,768]{3,2,1,0:T(8,128)(2,1)S(1)}, u32[]{:S(2)}, u32[]{:S(2)}) async-start(bf16[8,1,128,768]{3,2,1,0:T(8,128)(2,1)} %copy.25), calls=%async_computation | async-start | bytes 3145728 | tf_op jit(solution)/shard_map/all_to_all | solution.py:58
  11.7 0.0 copy-done.6
  11.7 0.1 pad.7.clone
  11.8 0.0 copy-done.5
  11.8 0.2 and_reduce_fusion
  12.0 20.6 %all-to-all-done = bf16[8,1,128,768]{3,2,1,0:T(8,128)(2,1)S(1)} async-done(((bf16[8,1,128,768]{3,2,1,0:T(8,128)(2,1)}), bf16[8,1,128,768]{3,2,1,0:T(8,128)(2,1)S(1)}, u32[]{:S(2)}, u32[]{:S(2)}) %all-to-all-start) | async-done | bytes 1572896 | tf_op jit(solution)/shard_map/all_to_all | solution.py:58
  32.7 0.4 convolution_convert_fusion.3
  33.1 0.1 fusion.23
  33.3 0.0 copy-start.2
  33.3 4.8 %collective-permute-start.1 = (bf16[528,256]{1,0:T(8,128)(2,1)S(1)}, bf16[528,256]{1,0:T(8,128)(2,1)S(1)}, u32[]{:S(2)}, u32[]{:S(2)}) collective-permute-start(bf16[528,256]{1,0:T(8,128)(2,1)S(1)} %get-tuple-element.20), channel_id=1, source_target_pairs={{0,32},{8,40},{16,48},{24,56},{32,64},{40,72},{48,80},{56,88},{64,... | collective-permute-start | bytes 811016 | tf_op jit(solution)/shard_map/ppermute | solution.py:14
  38.1 2.3 collective-permute-start
  40.4 5.0 %collective-permute-done.1 = bf16[528,256]{1,0:T(8,128)(2,1)S(1)} collective-permute-done((bf16[528,256]{1,0:T(8,128)(2,1)S(1)}, bf16[528,256]{1,0:T(8,128)(2,1)S(1)}, u32[]{:S(2)}, u32[]{:S(2)}) %collective-permute-start.1) | collective-permute-done | bytes 270368 | tf_op jit(solution)/shard_map/ppermute | solution.py:14
  45.4 0.0 copy-start.3
  45.4 7.1 %collective-permute-done = bf16[528,256]{1,0:T(8,128)(2,1)S(1)} collective-permute-done((bf16[528,256]{1,0:T(8,128)(2,1)S(1)}, bf16[528,256]{1,0:T(8,128)(2,1)S(1)}, u32[]{:S(2)}, u32[]{:S(2)}) %collective-permute-start) | collective-permute-done | bytes 270368 | tf_op jit(solution)/shard_map/ppermute | solution.py:14
  52.5 0.0 copy-start.4
  52.5 0.1 fusion.24
  52.6 0.1 collective-permute-start.2
  52.7 17.8 %collective-permute-done.2 = bf16[3,528,256]{2,1,0:T(8,128)(2,1)S(1)} collective-permute-done((bf16[3,528,256]{2,1,0:T(8,128)(2,1)S(1)}, bf16[3,528,256]{2,1,0:T(8,128)(2,1)S(1)}, u32[]{:S(2)}, u32[]{:S(2)}) %collective-permute-start.2) | collective-permute-done | bytes 811040 | tf_op jit(solution)/shard_map/ppermute | solution.py:91
  70.5 0.0 copy-done.2
  70.5 0.0 copy-done.3
  70.5 0.0 copy-done.4
  70.5 1.3 pad_maximum_fusion
  71.9 0.8 collective-permute-start.3
  72.7 3.1 %collective-permute-start.4 = (bf16[2,3,528,256]{3,2,1,0:T(8,128)(2,1)}, bf16[2,3,528,256]{3,2,1,0:T(8,128)(2,1)}, u32[]{:S(2)}, u32[]{:S(2)}) collective-permute-start(bf16[2,3,528,256]{3,2,1,0:T(8,128)(2,1)} %pad_maximum_fusion), channel_id=1, source_target_pairs={{0,4},{1,5},{2,6},{3,7},{4,0},{5,1},{6,2},{7,3},{8,12},{9,13},{10,... | collective-permute-start | bytes 4866056 | tf_op jit(solution)/shard_map/ppermute | solution.py:94
  75.8 0.0 collective-permute-start.5
  75.8 1.2 constant_dynamic-update-slice_fusion.4
  76.9 0.1 constant_dynamic-update-slice_fusion.3
  77.0 30.4 %collective-permute-done.3 = bf16[2,3,528,256]{3,2,1,0:T(8,128)(2,1)} collective-permute-done((bf16[2,3,528,256]{3,2,1,0:T(8,128)(2,1)}, bf16[2,3,528,256]{3,2,1,0:T(8,128)(2,1)}, u32[]{:S(2)}, u32[]{:S(2)}) %collective-permute-start.3) | collective-permute-done | bytes 1622048 | tf_op jit(solution)/shard_map/ppermute | solution.py:94
  107.4 1.5 constant_dynamic-update-slice_fusion.2
  108.9 0.1 collective-permute-done.4
  109.0 1.5 constant_dynamic-update-slice_fusion.1
  110.5 36.2 %collective-permute-done.5 = bf16[2,3,528,256]{3,2,1,0:T(8,128)(2,1)} collective-permute-done((bf16[2,3,528,256]{3,2,1,0:T(8,128)(2,1)}, bf16[2,3,528,256]{3,2,1,0:T(8,128)(2,1)}, u32[]{:S(2)}, u32[]{:S(2)}) %collective-permute-start.5) | collective-permute-done | bytes 1622048 | tf_op jit(solution)/shard_map/ppermute | solution.py:94
  146.8 1.5 constant_dynamic-update-slice_fusion.first_ref
  148.3 0.0 copy-start.1
  148.3 2.6 %constant_dynamic-slice_fusion = bf16[8,2,528,256]{3,2,1,0:T(8,128)(2,1)} fusion(bf16[8,3,528,256]{3,2,1,0:T(8,128)(2,1)S(1)} %constant_dynamic-update-slice_fusion.first_ref, s32[]{:T(128)S(6)} %select_n.52), kind=kLoop, calls=%fused_computation.77 | loop fusion | bytes 8650756 | tf_op jit(solution)/shard_map/dynamic_slice | solution.py:101
  150.9 1.4 copy-done.1
  152.3 0.5 collective-permute-start.6
  152.8 0.9 copy.30.qseg_ref
  153.7 0.6 fusion.26
  155.5 0.1 concatenate.23
  155.6 0.1 slice.69
  155.7 0.7 convolution_convert_fusion.1
  156.4 0.9 copy.29
  157.3 1.0 slice_reduce_fusion.7
  158.3 1.8 collective-permute-done.6.second_ref
  160.1 1.0 slice_reduce_fusion.5
  161.1 0.1 concatenate.28
  161.2 0.1 concatenate.27
  161.3 1.2 and_select_fusion.1
  162.5 0.6 concatenate.29.meta_ref
  163.1 99.8 %shard_map.55 = bf16[512,512]{1,0:T(8,128)(2,1)} custom-call(s32[81]{0:T(128)} %concatenate.29.meta_ref, bf16[512,512]{1,0:T(8,128)(2,1)} %bitcast.46, f32[512,1]{1,0:T(8,128)} %copy.30.qseg_ref, bf16[8,3,528,256]{3,2,1,0:T(8,128)(2,1)} %copy-done.1, bf16[8,2,528,256]{3,2,1,0:T(8,128)(2,1)} %collective-permute-done.6.second_ref), custom_call_target="tpu_custom_call" | custom-call | flops 21474836480 | bytes 11862016 | tf_op jit(solution)/shard_map/pallas_call | solution.py:227
  (12 shorter events, 0.2 us)
Async XLA Ops:
  0.0 4.0 %copy-start = (bf16[1024,512]{1,0:T(8,128)(2,1)S(1)}, bf16[1024,512]{1,0:T(8,128)(2,1)}, u32[]{:S(2)}) copy-start(bf16[1024,512]{1,0:T(8,128)(2,1)} %param.5) | copy-start | bytes 3145732
  4.9 6.8 %copy-start.6 = (s32[512]{0:T(512)S(1)}, s32[512]{0:T(512)}, u32[]{:S(2)}) copy-start(s32[512]{0:T(512)} %param.9) | copy-start | bytes 6148
  4.9 6.9 %copy-start.5 = (s32[8,8]{1,0:T(8,128)S(1)}, s32[8,8]{1,0:T(8,128)}, u32[]{:S(2)}) copy-start(s32[8,8]{1,0:T(8,128)} %param.7) | copy-start | bytes 772
  6.3 26.3 %all-to-all-start = ((bf16[8,1,128,768]{3,2,1,0:T(8,128)(2,1)}), bf16[8,1,128,768]{3,2,1,0:T(8,128)(2,1)S(1)}, u32[]{:S(2)}, u32[]{:S(2)}) async-start(bf16[8,1,128,768]{3,2,1,0:T(8,128)(2,1)} %copy.25), calls=%async_computation | async-start | bytes 3145728 | tf_op jit(solution)/shard_map/all_to_all | solution.py:58
  33.3 37.3 %copy-start.2 = (bf16[1,528,256]{2,1,0:T(8,128)(2,1)}, bf16[1,528,256]{2,1,0:T(8,128)(2,1)S(1)}, u32[]{:S(2)}) copy-start(bf16[1,528,256]{2,1,0:T(8,128)(2,1)S(1)} %get-tuple-element.19) | copy-start | bytes 811012
  33.3 12.1 %collective-permute-start.1 = (bf16[528,256]{1,0:T(8,128)(2,1)S(1)}, bf16[528,256]{1,0:T(8,128)(2,1)S(1)}, u32[]{:S(2)}, u32[]{:S(2)}) collective-permute-start(bf16[528,256]{1,0:T(8,128)(2,1)S(1)} %get-tuple-element.20), channel_id=1, source_target_pairs={{0,32},{8,40},{16,48},{24,56},{32,64},{40,72},{48,80},{56,88},{64,... | collective-permute-start | bytes 811016 | tf_op jit(solution)/shard_map/ppermute | solution.py:14
  38.1 14.4 %collective-permute-start = (bf16[528,256]{1,0:T(8,128)(2,1)S(1)}, bf16[528,256]{1,0:T(8,128)(2,1)S(1)}, u32[]{:S(2)}, u32[]{:S(2)}) collective-permute-start(bf16[528,256]{1,0:T(8,128)(2,1)S(1)} %get-tuple-element.20), channel_id=1, source_target_pairs={{0,16},{8,24},{16,32},{24,40},{32,48},{40,56},{48,64},{56,72},{64,... | collective-permute-start | bytes 811016 | tf_op jit(solution)/shard_map/ppermute | solution.py:14
  45.4 25.1 %copy-start.3 = (bf16[528,256]{1,0:T(8,128)(2,1)}, bf16[528,256]{1,0:T(8,128)(2,1)S(1)}, u32[]{:S(2)}) copy-start(bf16[528,256]{1,0:T(8,128)(2,1)S(1)} %collective-permute-done.1) | copy-start | bytes 811012
  52.5 18.0 %copy-start.4 = (bf16[528,256]{1,0:T(8,128)(2,1)}, bf16[528,256]{1,0:T(8,128)(2,1)S(1)}, u32[]{:S(2)}) copy-start(bf16[528,256]{1,0:T(8,128)(2,1)S(1)} %collective-permute-done) | copy-start | bytes 811012
  52.6 17.9 %collective-permute-start.2 = (bf16[3,528,256]{2,1,0:T(8,128)(2,1)S(1)}, bf16[3,528,256]{2,1,0:T(8,128)(2,1)S(1)}, u32[]{:S(2)}, u32[]{:S(2)}) collective-permute-start(bf16[3,528,256]{2,1,0:T(8,128)(2,1)S(1)} %get-tuple-element.18), channel_id=1, source_target_pairs={{0,1},{1,0},{2,3},{3,2},{4,5},{5,4},{6,7},{7,6},{8,9},{9,8},{10,11... | collective-permute-start | bytes 2433032 | tf_op jit(solution)/shard_map/ppermute | solution.py:91
  71.9 35.6 %collective-permute-start.3 = (bf16[2,3,528,256]{3,2,1,0:T(8,128)(2,1)}, bf16[2,3,528,256]{3,2,1,0:T(8,128)(2,1)}, u32[]{:S(2)}, u32[]{:S(2)}) collective-permute-start(bf16[2,3,528,256]{3,2,1,0:T(8,128)(2,1)} %pad_maximum_fusion), channel_id=1, source_target_pairs={{0,2},{1,3},{2,4},{3,5},{4,6},{5,7},{6,0},{7,1},{8,10},{9,11},{10,... | collective-permute-start | bytes 4866056 | tf_op jit(solution)/shard_map/ppermute | solution.py:94
  72.7 36.3 %collective-permute-start.4 = (bf16[2,3,528,256]{3,2,1,0:T(8,128)(2,1)}, bf16[2,3,528,256]{3,2,1,0:T(8,128)(2,1)}, u32[]{:S(2)}, u32[]{:S(2)}) collective-permute-start(bf16[2,3,528,256]{3,2,1,0:T(8,128)(2,1)} %pad_maximum_fusion), channel_id=1, source_target_pairs={{0,4},{1,5},{2,6},{3,7},{4,0},{5,1},{6,2},{7,3},{8,12},{9,13},{10,... | collective-permute-start | bytes 4866056 | tf_op jit(solution)/shard_map/ppermute | solution.py:94
  75.8 71.0 %collective-permute-start.5 = (bf16[2,3,528,256]{3,2,1,0:T(8,128)(2,1)}, bf16[2,3,528,256]{3,2,1,0:T(8,128)(2,1)}, u32[]{:S(2)}, u32[]{:S(2)}) collective-permute-start(bf16[2,3,528,256]{3,2,1,0:T(8,128)(2,1)} %pad_maximum_fusion), channel_id=1, source_target_pairs={{0,6},{1,7},{2,0},{3,1},{4,2},{5,3},{6,4},{7,5},{8,14},{9,15},{10,... | collective-permute-start | bytes 4866056 | tf_op jit(solution)/shard_map/ppermute | solution.py:94
  148.3 4.0 %copy-start.1 = (bf16[8,3,528,256]{3,2,1,0:T(8,128)(2,1)}, bf16[8,3,528,256]{3,2,1,0:T(8,128)(2,1)S(1)}, u32[]{:S(2)}) copy-start(bf16[8,3,528,256]{3,2,1,0:T(8,128)(2,1)S(1)} %constant_dynamic-update-slice_fusion.first_ref) | copy-start | bytes 19464196
  152.3 7.8 %collective-permute-start.6 = (bf16[8,2,528,256]{3,2,1,0:T(8,128)(2,1)}, bf16[8,2,528,256]{3,2,1,0:T(8,128)(2,1)}, u32[]{:S(2)}, u32[]{:S(2)}) collective-permute-start(bf16[8,2,528,256]{3,2,1,0:T(8,128)(2,1)} %constant_dynamic-slice_fusion), channel_id=1, source_target_pairs={{0,8},{8,0},{16,24},{24,16},{32,40},{40,32},{48,56},{56,48},{64,72... | collective-permute-start | bytes 12976136 | tf_op jit(solution)/shard_map/ppermute | solution.py:104
